TPU v7x, 256 devices: a whole 4x4x8 slice. The times are simulated.
256 devices in a mesh: section: 16 (over z_lo, y, core), tensor: 16 (over x, z_hi).
Axes of the slice: x: 4, y: 4, z: 8 (z_hi: 4, z_lo: 2; z = z_hi * 2 + z_lo), core: 2. Of those that a mesh axis runs over, the one named last changes fastest.
Arguments:
- hidden: bfloat16 [16, 64, 8192], P('section'), may hold values from -14 to 14
- head: bfloat16 [8192, 65536], P('section', 'tensor'), may hold values from -0.25 to 0.25
- exit_loss_weight: float32 [16], P('section'), may hold values from 2 to 32
Outputs:
- grad_hidden: float32 [1024, 8192], P('tensor', 'section')
- grad_head: bfloat16 [8192, 65536], P('section', 'tensor')
All inputs are finite; a program needn't handle non-finite values.
Results may differ from a plain program's by a relative error of at most 0.011.
Values may be sent and summed in bfloat16 or wider, within the bound.
No kernel may reach another device: no remote copies, remote signals or barrier semaphores. Data moves between devices by JAX's collectives and lax.ppermute only.
A program may use at most 128 MiB of HBM per device.

v0:
```python
import jax
import jax.numpy as jnp
from jax import lax
from jax.sharding import PartitionSpec as P

scaling_divisor = 2.0


def from_root(value, axis, source):
    kept = jnp.where(lax.axis_index(axis) == source, value, 0).astype(value.dtype)
    return lax.psum(kept, axis)


def local(hidden, head, exit_loss_weight):
    departure_number = lax.axis_size("section")
    tok_count = hidden.shape[1]
    row_count = departure_number * tok_count
    local_cols = lax.all_to_all(hidden, "section", split_axis=2, concat_axis=0, tiled=True)
    flat_hidden = local_cols.reshape(row_count, local_cols.shape[2])
    own_logits = lax.psum_scatter(
        jnp.dot(flat_hidden, head, preferred_element_type=jnp.float32),
        "section",
        scatter_dimension=0,
        tiled=True,
    )
    mentor_score_matrix = from_root(own_logits, "section", departure_number - 1)
    mentor_distribution = mentor_score_matrix / scaling_divisor
    local_smax = jnp.max(own_logits, axis=1)
    local_tmax = jnp.max(mentor_distribution, axis=1)
    student_max, teacher_max = lax.pmax((local_smax, local_tmax), "tensor")
    student_sum, teacher_sum = lax.psum(
        (
            jnp.sum(jnp.exp(own_logits - student_max[:, None]), axis=1),
            jnp.sum(jnp.exp(mentor_distribution - teacher_max[:, None]), axis=1),
        ),
        "tensor",
    )
    student_norm = student_max + jnp.log(student_sum)
    teacher_norm = teacher_max + jnp.log(teacher_sum)
    log_student = own_logits - student_norm[:, None]
    log_teacher = mentor_distribution - teacher_norm[:, None]
    log_mixture = jnp.logaddexp(log_student, log_teacher) - jnp.log(2.0)
    midpoint_difference = 0.5 * (log_student - log_mixture)
    student = jnp.exp(log_student)
    average = lax.psum(jnp.sum(student * midpoint_difference, axis=1), "tensor")
    grad_logits = (exit_loss_weight[0] * student * (midpoint_difference - average[:, None])).astype(
        jnp.bfloat16
    )
    piece = lax.all_gather(grad_logits, "section", axis=0, tiled=True)
    head_grad = lax.dot_general(
        flat_hidden, piece, (((0,), (0,)), ((), ())), preferred_element_type=jnp.float32
    )
    row_grad = lax.dot_general(
        piece, head, (((1,), (1,)), ((), ())), preferred_element_type=jnp.float32
    )
    hidden_part = row_grad
    head_grad, hidden_part = (head_grad, hidden_part)
    grad_hidden = lax.psum_scatter(hidden_part, "tensor", scatter_dimension=0, tiled=True)
    return (grad_hidden, head_grad.astype(jnp.bfloat16))


def solution(mesh):
    placed = (P("section", None, None), P("section", "tensor"), P("section"))
    return jax.shard_map(
        local,
        mesh=mesh,
        in_specs=placed,
        out_specs=(P("tensor", "section"), P("section", "tensor")),
        check_vma=False,
    )
```

profile of v0, /device:TPU:8, one launch (start us, length us, event | category | flops | bytes accessed | tf_op | source)
XLA Modules:
  0.0 624.9 jit_solution(6586606897295019781)
XLA Ops:
  7.2 0.0 reduce-scatter.3.cloned.1.call-start
  7.2 9.2 %copy.9 = bf16[1,64,8192]{1,0,2:T(2,128)(2,1)} copy(bf16[1,64,8192]{2,1,0:T(8,128)(2,1)} %param.3) | data formatting | bytes 2097152 | tf_op args[0]
  16.4 0.5 broadcast.12
  16.9 45.2 %reduce = bf16[8192,64]{1,0:T(8,128)(2,1)S(1)} reduce(bf16[8192,1,64]{2,1,0:T(2,128)(2,1)} %bitcast.21, bf16[]{:T(256)} %broadcast.12), dimensions={1}, to_apply=%bitcast.11.reduce_sub_computation | reduce | bytes 2097154
  62.1 1.5 reshape.14
  63.6 19.1 %all_to_all.15 = bf16[16,2,16384]{2,1,0:T(2,128)(2,1)S(1)} all-to-all(bf16[16,2,16384]{2,1,0:T(2,128)(2,1)S(1)} %reshape.14), channel_id=1, replica_groups=mesh['section'=16,'tensor'=16] {'section'}, dimensions={0} | all-to-all | bytes 2097152 | tf_op jit(solution)/shard_map/all_to_all | solution.py:18
  82.7 7.0 %reshape.15 = bf16[8192,1,64]{2,1,0:T(2,128)(2,1)} reshape(bf16[16,2,16384]{2,1,0:T(2,128)(2,1)S(1)} %all_to_all.15) | data formatting | bytes 2097152
  89.7 8.2 %copy.10 = bf16[1,64,8192]{2,1,0:T(8,128)(2,1)S(1)} copy(bf16[1,64,8192]{1,0,2:T(2,128)(2,1)} %bitcast.22) | data formatting | bytes 2097152 | tf_op jit(solution)/shard_map/all_to_all | solution.py:18
  97.8 0.0 copy-start.2
  97.8 0.4 copy.13
  98.2 0.1 bitcast_bitcast_fusion
  98.3 0.6 copy.11
  98.9 1.2 copy-done.2
  100.0 8.1 %fusion.2 = f32[1024,4096]{1,0:T(8,128)} fusion(bf16[1024,512]{1,0:T(8,128)(2,1)S(1)} %bitcast.25, bf16[512,4096]{1,0:T(8,128)(2,1)S(1)} %copy-done.2), kind=kOutput, calls=%fused_computation.13 | convolution fusion | flops 4294967296 | bytes 22020096 | tf_op jit(solution)/shard_map/dot_general | solution.py:21
  108.1 0.0 reduce-scatter.3.cloned.1.call-update
  108.1 0.0 all-reduce.4.cloned.1.call-start
  108.2 100.5 %reduce-scatter.3.cloned.1.call-done = f32[64,4096]{1,0:T(8,128)} async-done(((f32[1024,4096]{1,0:T(8,128)}), f32[64,4096]{1,0:T(8,128)}) %reduce-scatter.3.cloned.1.call-update) | async-done | bytes 1048592 | tf_op jit(solution)/shard_map/reduce_scatter | solution.py:20
  208.6 0.0 copy-start.1
  208.6 2.5 fusion.1
  211.1 0.0 all-reduce.4.cloned.1.call-update
  211.1 0.0 all-gather.2.cloned.1.call-start
  211.8 122.8 %all-reduce.4.cloned.1.call-done = f32[64,4096]{1,0:T(8,128)} async-done(((f32[64,4096]{1,0:T(8,128)}), f32[64,4096]{1,0:T(8,128)}) %all-reduce.4.cloned.1.call-update) | async-done | bytes 1048592 | tf_op jit(solution)/shard_map/psum | solution.py:11
  334.6 0.0 copy-start
  334.6 1.5 multiply_reduce_fusion.1
  336.1 45.0 %all-reduce.1 = (f32[64]{0:T(128)S(1)}, f32[64]{0:T(128)S(1)}) all-reduce(f32[64]{0:T(128)S(1)} %multiply_reduce_fusion.1, f32[64]{0:T(128)S(1)} %get-tuple-element.14), channel_id=1, replica_groups=mesh['section'=16,'tensor'=16] {'tensor'}, use_global_device_ids=true, to_apply=%region_7.8 | all-reduce | flops 128 | bytes 1024 | tf_op jit(solution)/shard_map/pmax | solution.py:30
  381.1 0.0 copy-done.1
  381.1 1.7 exponential_reduce_fusion
  382.8 39.2 %all-reduce = (f32[64]{0:T(128)S(1)}, f32[64]{0:T(128)S(1)}) all-reduce(f32[64]{0:T(128)S(1)} %get-tuple-element.16, f32[64]{0:T(128)S(1)} %get-tuple-element.17), channel_id=1, replica_groups=mesh['section'=16,'tensor'=16] {'tensor'}, use_global_device_ids=true, to_apply=%region_9.10 | all-reduce | flops 128 | bytes 1024 | tf_op jit(solution)/shard_map/psum | solution.py:31
  422.1 2.4 multiply_reduce_fusion
  424.4 42.0 %psum.31 = f32[64]{0:T(128)S(1)} all-reduce(f32[64]{0:T(128)S(1)} %multiply_reduce_fusion), channel_id=1, replica_groups=mesh['section'=16,'tensor'=16] {'tensor'}, use_global_device_ids=true, to_apply=%region_11.12 | all-reduce | flops 64 | bytes 512 | tf_op jit(solution)/shard_map/psum | solution.py:45
  466.4 0.0 copy-done
  466.4 1.9 multiply_convert_fusion
  468.3 0.0 all-gather.2.cloned.1.call-update
  468.3 0.0 reduce-scatter.5.cloned.1.call-start
  468.4 49.5 %all-gather.2.cloned.1.call-done = bf16[1024,4096]{1,0:T(8,128)(2,1)} async-done(((bf16[64,4096]{1,0:T(8,128)(2,1)}), bf16[1024,4096]{1,0:T(8,128)(2,1)}) %all-gather.2.cloned.1.call-update) | async-done | bytes 8388624 | tf_op jit(solution)/shard_map/all_gather | solution.py:49
  517.9 10.5 %fusion.3 = f32[1024,512]{1,0:T(8,128)} fusion(bf16[1024,4096]{1,0:T(8,128)(2,1)} %all-gather.2.cloned.1.call-done, bf16[512,4096]{1,0:T(8,128)(2,1)} %param.4), kind=kOutput, calls=%fused_computation.14 | convolution fusion | flops 4294967296 | bytes 14680064 | tf_op jit(solution)/shard_map/dot_general | solution.py:53
  528.3 0.0 reduce-scatter.5.cloned.1.call-update
  528.4 9.8 %fusion = bf16[512,4096]{0,1:T(8,128)(2,1)} fusion(bf16[1024,4096]{1,0:T(8,128)(2,1)} %all-gather.2.cloned.1.call-done, bf16[1024,512]{1,0:T(8,128)(2,1)S(1)} %bitcast.26), kind=kOutput, calls=%fused_computation.1 | convolution fusion | flops 4297064448 | bytes 13631488 | tf_op jit(solution)/shard_map/dot_general | solution.py:50
  538.1 6.3 %copy.12 = bf16[512,4096]{1,0:T(8,128)(2,1)} copy(bf16[512,4096]{0,1:T(8,128)(2,1)} %fusion) | data formatting | bytes 8388608
  544.4 73.9 %reduce-scatter.5.cloned.1.call-done = f32[64,512]{1,0:T(8,128)} async-done(((f32[1024,512]{1,0:T(8,128)}), f32[64,512]{1,0:T(8,128)}) %reduce-scatter.5.cloned.1.call-update) | async-done | bytes 131088 | tf_op jit(solution)/shard_map/reduce_scatter | solution.py:58
  (2 shorter events, 0.0 us)
Async XLA Ops:
  7.2 201.4 %reduce-scatter.3.cloned.1.call-start = ((), (), s32[]{:S(2)}) async-start(), calls=%async_computation.3 | async-start | bytes 17825792 | tf_op jit(solution)/shard_map/reduce_scatter | solution.py:20
  97.8 2.2 copy-start.2
  108.1 226.5 %all-reduce.4.cloned.1.call-start = ((), (), s32[]{:S(2)}) async-start(), calls=%async_computation.4 | async-start | bytes 2097152 | tf_op jit(solution)/shard_map/psum | solution.py:11
  208.6 172.5 %copy-start.1 = (f32[64,4096]{1,0:T(8,128)S(1)}, f32[64,4096]{1,0:T(8,128)}, u32[]{:S(2)}) copy-start(f32[64,4096]{1,0:T(8,128)} %reduce-scatter.3.cloned.1.call-done) | copy-start | bytes 3145732
  211.1 306.8 %all-gather.2.cloned.1.call-start = ((), (), s32[]{:S(2)}) async-start(), calls=%async_computation.5 | async-start | bytes 8912896 | tf_op jit(solution)/shard_map/all_gather | solution.py:49
  334.6 131.8 %copy-start = (f32[64,4096]{1,0:T(8,128)S(1)}, f32[64,4096]{1,0:T(8,128)}, u32[]{:S(2)}) copy-start(f32[64,4096]{1,0:T(8,128)} %all-reduce.4.cloned.1.call-done) | copy-start | bytes 3145732
  468.3 150.0 %reduce-scatter.5.cloned.1.call-start = ((), (), s32[]{:S(2)}) async-start(), calls=%async_computation.6 | async-start | bytes 2228224 | tf_op jit(solution)/shard_map/reduce_scatter | solution.py:58
Sparse Core Ops, SparseCore 0:
  108.2 100.3 reduce-scatter.2
  211.8 122.7 all-reduce.3
  468.5 49.3 all-gather.1
  528.5 89.8 reduce-scatter.4
where the time goes:
time: 626 us; the launch traced here: 625 us
  waiting for transfers between devices  347 us (55%)
  blocking collectives  145 us (23%)
  other arithmetic  55.1 us (9%)
  local copies, waits for them, and re-layouts  34.7 us (6%)
  matrix products  28.3 us (5%)
  between operations  14.5 us (2%)
    psum x1, waiting for transfers between devices, from_root(): return lax.psum(kept, axis)  123 us
    reduce_scatter x1, waiting for transfers between devices, local(): lax.psum_scatter(jnp.dot(flat_hidden, head, preferred_element_type=jnp.fl...  100 us
    reduce_scatter x1, waiting for transfers between devices, local(): lax.psum_scatter(hidden_part, 'tensor', scatter_dimension=0, tiled=True)  73.9 us
    all_gather x1, waiting for transfers between devices, local(): piece = lax.all_gather(grad_logits, 'section', axis=0, tiled=True)  49.5 us
    unnamed x1, other arithmetic  45.2 us
    pmax x1, blocking collectives, local(): student_max, teacher_max = lax.pmax((local_smax, local_tmax), 'tensor')  45 us
    psum x1, blocking collectives, local(): average = lax.psum(jnp.sum(student * midpoint_difference, axis=1), 'tensor')  42 us
    psum x1, blocking collectives, local(): lax.psum((jnp.sum(jnp.exp(own_logits - student_max[:, None]), axis=1), jn...  39.2 us
  transfers between devices with their start and end apart: 4, of which 4 were waited for; matrix products, arithmetic and copies ran while one was open for 3% of the time, Pallas kernels for 0%

commit v1 on v0

v1 whole, which is shorter than its diff:
```python
import math

import jax
import jax.numpy as jnp
from jax import lax
from jax.sharding import PartitionSpec as P

scaling_divisor = 2.0


def _lse(x, axes):
    top = jnp.max(x, axis=axes, keepdims=True)
    return top + jnp.log(jnp.sum(jnp.exp(x - top), axis=axes, keepdims=True))


def local(hidden, head, exit_loss_weight):
    sections = lax.axis_size("section")
    tensors = lax.axis_size("tensor")
    _, tok, width = hidden.shape
    exits = sections
    dblk = width // sections
    vblk = head.shape[1]
    tps = tok // sections
    n_eq = tensors // tps
    kpe = exits // n_eq

    x = hidden[0].reshape(tok, sections, dblk).transpose(1, 0, 2)
    cols = lax.all_to_all(x, "section", 0, 0, tiled=True)
    lhs = cols.reshape(exits, sections, tps, dblk).transpose(1, 0, 2, 3)
    lhs = lhs.reshape(sections * exits * tps, dblk)
    part = jnp.dot(lhs, head, preferred_element_type=jnp.float32)
    own = lax.psum_scatter(part, "section", scatter_dimension=0, tiled=True)
    own = own.reshape(n_eq, kpe, tps, vblk)
    stud = own.transpose(2, 0, 1, 3).reshape(tensors, kpe, vblk)
    teach = jnp.broadcast_to(own[n_eq - 1, kpe - 1][:, None, None, :], (tps, n_eq, 1, vblk))
    send = jnp.concatenate([stud, teach.reshape(tensors, 1, vblk)], axis=1)
    rows = lax.all_to_all(send, "tensor", 0, 0, tiled=True)

    logits = rows[:, :kpe, :]
    teacher = rows[:, kpe, :] / scaling_divisor
    log_student = logits - _lse(logits, (0, 2))
    log_teacher = teacher - _lse(teacher, (0, 1))
    log_mixture = jnp.logaddexp(log_student, log_teacher[:, None, :]) - jnp.log(2.0)
    halfgap = 0.5 * (log_student - log_mixture)
    student = jnp.exp(log_student)
    average = jnp.sum(student * halfgap, axis=(0, 2), keepdims=True)

    weights = lax.all_gather(exit_loss_weight, "section", axis=0, tiled=True)
    eq = lax.rem(lax.axis_index("tensor"), n_eq)
    wk = lax.dynamic_slice(weights, (eq * kpe,), (kpe,))
    grad_logits = (wk[None, :, None] * student * (halfgap - average)).astype(jnp.bfloat16)

    back = lax.all_to_all(grad_logits, "tensor", 0, 0, tiled=True)
    back = back.reshape(tps, exits, vblk)
    piece = lax.all_gather(back, "section", axis=0, tiled=True)

    head_grad = lax.dot_general(
        cols, piece, (((0, 1), (1, 0)), ((), ())), preferred_element_type=jnp.float32
    )
    row_grad = lax.dot_general(
        piece, head, (((2,), (1,)), ((), ())), preferred_element_type=jnp.float32
    )
    grad_hidden = lax.psum_scatter(row_grad, "tensor", scatter_dimension=1, tiled=True)
    grad_hidden = grad_hidden.reshape(tok, dblk)
    return (grad_hidden, head_grad.astype(jnp.bfloat16))


def solution(mesh):
    placed = (P("section", None, None), P("section", "tensor"), P("section"))
    return jax.shard_map(
        local,
        mesh=mesh,
        in_specs=placed,
        out_specs=(P("tensor", "section"), P("section", "tensor")),
        check_vma=False,
    )
```

time: 626 us -> 418 us (0.67)
  waiting for transfers between devices: 347 us -> 229 us
  other arithmetic: 55.1 us -> 9.26 us
  blocking collectives: 145 us -> 107 us
  local copies, waits for them, and re-layouts: 34.7 us -> 17.2 us
  starting transfers between devices: 0.16 us -> 9.89 us
    psum x1 -> x0, waiting for transfers between devices: 123 us -> none  [from_root(): return lax.psum(kept, axis)]
    psum x2 -> x0, blocking collectives: 81.2 us -> none  [the longest x1 42 us: local(): average = lax.psum(jnp.sum(student * midpoint_difference, axis=1), 'tensor')]
    unnamed x0 -> x1, blocking collectives: none -> 65.7 us
    unnamed x1 -> x0, other arithmetic: 45.2 us -> none
    pmax x1 -> x0, blocking collectives: 45 us -> none  [local(): student_max, teacher_max = lax.pmax((local_smax, local_tmax), 'tensor')]
    all_to_all x1 -> x2, blocking collectives: 19.1 us -> 41.6 us  [the longest x1 22.5 us: local(): back = lax.all_to_all(grad_logits, 'tensor', 0, 0, tiled=True)]
    unnamed x12 -> x8, local copies, waits for them, and re-layouts: 25.9 us -> 9.4 us
    all_to_all x0 -> x1, starting transfers between devices: none -> 9.77 us  [local(): rows = lax.all_to_all(send, 'tensor', 0, 0, tiled=True)]
  transfers between devices with their start and end apart: 4 -> 4, of which waited for: 4 -> 3; matrix products, arithmetic and copies ran while one was open for 3% -> 4% of each run, Pallas kernels for 0% -> 0%
where the time goes in v1:
time: 418 us; the launch traced here: 417 us
  waiting for transfers between devices  229 us (55%)
  blocking collectives  107 us (26%)
  matrix products  28.7 us (7%)
  local copies, waits for them, and re-layouts  17.2 us (4%)
  between operations  15.9 us (4%)
  starting transfers between devices  9.89 us (2%)
  other arithmetic  9.26 us (2%)
    reduce_scatter x1, waiting for transfers between devices, local(): own = lax.psum_scatter(part, 'section', scatter_dimension=0, tiled=True)  101 us
    reduce_scatter x1, waiting for transfers between devices, local(): lax.psum_scatter(row_grad, 'tensor', scatter_dimension=1, tiled=True)  73.4 us
    unnamed x1, blocking collectives  65.7 us
    all_gather x1, waiting for transfers between devices, local(): piece = lax.all_gather(back, 'section', axis=0, tiled=True)  55.2 us
    all_to_all x1, blocking collectives, local(): back = lax.all_to_all(grad_logits, 'tensor', 0, 0, tiled=True)  22.5 us
    all_to_all x1, blocking collectives, local(): cols = lax.all_to_all(x, 'section', 0, 0, tiled=True)  19.1 us
    dot_general x1, matrix products, local(): part = jnp.dot(lhs, head, preferred_element_type=jnp.float32)  10.3 us
    dot_general x1, matrix products, local(): lax.dot_general(cols, piece, (((0, 1), (1, 0)), ((), ())), preferred_elem...  10.3 us
  transfers between devices with their start and end apart: 4, of which 3 were waited for; matrix products, arithmetic and copies ran while one was open for 4% of the time, Pallas kernels for 0%

profile of v1, /device:TPU:8, one launch (start us, length us, event | category | flops | bytes accessed | tf_op | source)
XLA Modules:
  0.0 417.4 jit_solution(13925574629700191505)
XLA Ops:
  7.2 0.0 reduce-scatter.3.cloned.1.call-start
  7.2 1.6 copy.23
  8.8 0.6 copy.16
  9.4 19.1 %all_to_all.15 = bf16[16,64,512]{2,1,0:T(8,128)(2,1)S(1)} all-to-all(bf16[16,64,512]{2,1,0:T(8,128)(2,1)S(1)} %copy.16), channel_id=1, replica_groups=mesh['section'=16,'tensor'=16] {'section'}, dimensions={0} | all-to-all | bytes 2097152 | tf_op jit(solution)/shard_map/all_to_all | solution.py:28
  28.5 0.3 reshape.49
  28.8 0.5 copy.28
  29.3 0.3 reshape.50
  29.6 10.3 %fusion.5 = f32[1024,4096]{1,0:T(8,128)} fusion(bf16[1024,512]{1,0:T(8,128)(2,1)S(1)} %reshape.50, bf16[512,4096]{1,0:T(8,128)(2,1)} %param.4), kind=kOutput, calls=%fused_computation.20 | convolution fusion | flops 4294967296 | bytes 22020096 | tf_op jit(solution)/shard_map/dot_general | solution.py:31
  39.8 0.0 reduce-scatter.3.cloned.1.call-update
  39.9 100.5 %reduce-scatter.3.cloned.1.call-done = f32[64,4096]{1,0:T(8,128)} async-done(((f32[1024,4096]{1,0:T(8,128)}), f32[64,4096]{1,0:T(8,128)}) %reduce-scatter.3.cloned.1.call-update) | async-done | bytes 1048592 | tf_op jit(solution)/shard_map/reduce_scatter | solution.py:32
  140.4 1.5 reshape.51
  141.9 0.7 copy.18
  142.6 0.0 copy-start
  142.7 0.4 broadcast_in_dim.8
  143.0 1.7 pad_maximum_fusion
  144.8 9.8 %all-to-all-start.1 = ((f32[16,5,4096]{2,1,0:T(8,128)}), f32[16,5,4096]{2,1,0:T(8,128)S(1)}, u32[]{:S(2)}, u32[]{:S(2)}) async-start(f32[16,5,4096]{2,1,0:T(8,128)} %pad_maximum_fusion), calls=%async_computation.2 | async-start | bytes 4194304 | tf_op jit(solution)/shard_map/all_to_all | solution.py:37
  154.6 0.0 all-gather.2.cloned.1.call-start
  155.3 0.0 copy-done
  155.3 0.6 dynamic-slice
  155.9 0.8 dynamic-update-slice
  156.6 65.7 %all-reduce = f32[16]{0:T(128)S(1)} all-reduce(f32[16]{0:T(128)S(1)} %dynamic-update-slice), channel_id=1, replica_groups=mesh['section'=16,'tensor'=16] {'section'}, use_global_device_ids=true, to_apply=%add | all-reduce | flops 16 | bytes 128
  222.3 0.1 dynamic_slice.3
  222.4 0.0 all-to-all-done.1
  222.4 1.1 fusion.4
  223.5 1.8 exponential_reduce_fusion.1
  226.6 0.3 broadcast_subtract_fusion
  227.0 0.2 copy.29
  227.1 0.7 slice_reduce_fusion
  227.8 0.7 exponential_reduce_fusion
  228.6 2.2 multiply_reduce_fusion
  230.8 0.6 multiply_convert_fusion
  231.4 22.5 %all_to_all.16 = bf16[16,4,4096]{2,1,0:T(4,128)(2,1)S(1)} all-to-all(bf16[16,4,4096]{2,1,0:T(4,128)(2,1)S(1)} %multiply_convert_fusion), channel_id=1, replica_groups=mesh['section'=16,'tensor'=16] {'tensor'}, dimensions={0} | all-to-all | bytes 1048576 | tf_op jit(solution)/shard_map/all_to_all | solution.py:53
  253.9 0.9 reshape.53
  254.8 0.0 all-gather.2.cloned.1.call-update
  254.8 0.0 reduce-scatter.5.cloned.1.call-start
  254.9 55.2 %all-gather.2.cloned.1.call-done = bf16[64,16,4096]{2,1,0:T(8,128)(2,1)} async-done(((bf16[4,16,4096]{2,1,0:T(8,128)(2,1)}), bf16[64,16,4096]{2,1,0:T(8,128)(2,1)}) %all-gather.2.cloned.1.call-update) | async-done | bytes 8388624 | tf_op jit(solution)/shard_map/all_gather | solution.py:55
  310.1 8.2 %fusion.1 = f32[64,16,512]{2,1,0:T(8,128)S(1)} fusion(bf16[64,16,4096]{2,1,0:T(8,128)(2,1)} %all-gather.2.cloned.1.call-done, bf16[512,4096]{1,0:T(8,128)(2,1)} %param.4), kind=kOutput, calls=%fused_computation.2 | convolution fusion | flops 4294967296 | bytes 14680064 | tf_op jit(solution)/shard_map/dot_general | solution.py:60
  318.3 2.6 copy.19
  320.9 0.0 reduce-scatter.5.cloned.1.call-update
  320.9 10.3 %fusion = bf16[512,4096]{0,1:T(8,128)(2,1)} fusion(bf16[64,16,4096]{2,1,0:T(8,128)(2,1)} %all-gather.2.cloned.1.call-done, bf16[16,64,512]{2,1,0:T(8,128)(2,1)S(1)} %all_to_all.15), kind=kOutput, calls=%fused_computation.1 | convolution fusion | flops 4297064448 | bytes 13631488 | tf_op jit(solution)/shard_map/dot_general | solution.py:57
  331.1 6.3 %copy.21 = bf16[512,4096]{1,0:T(8,128)(2,1)} copy(bf16[512,4096]{0,1:T(8,128)(2,1)} %fusion) | data formatting | bytes 8388608
  337.5 73.4 %reduce-scatter.5.cloned.1.call-done = f32[64,1,512]{2,0,1:T(8,128)} async-done(((f32[64,16,512]{2,0,1:T(8,128)}), f32[64,1,512]{2,0,1:T(8,128)}) %reduce-scatter.5.cloned.1.call-update) | async-done | bytes 131088 | tf_op jit(solution)/shard_map/reduce_scatter | solution.py:63
  (4 shorter events, 0.1 us)
Async XLA Ops:
  7.2 133.2 %reduce-scatter.3.cloned.1.call-start = ((), (), s32[]{:S(2)}) async-start(), calls=%async_computation.5 | async-start | bytes 17825792 | tf_op jit(solution)/shard_map/reduce_scatter | solution.py:32
  142.6 12.7 %copy-start = (u32[256]{0:T(256)S(1)}, u32[256]{0:T(256)}, u32[]{:S(2)}) copy-start(u32[256]{0:T(256)} %constant.28) | copy-start | bytes 3076
  144.8 77.6 %all-to-all-start.1 = ((f32[16,5,4096]{2,1,0:T(8,128)}), f32[16,5,4096]{2,1,0:T(8,128)S(1)}, u32[]{:S(2)}, u32[]{:S(2)}) async-start(f32[16,5,4096]{2,1,0:T(8,128)} %pad_maximum_fusion), calls=%async_computation.2 | async-start | bytes 4194304 | tf_op jit(solution)/shard_map/all_to_all | solution.py:37
  154.6 155.5 %all-gather.2.cloned.1.call-start = ((), (), s32[]{:S(2)}) async-start(), calls=%async_computation.6 | async-start | bytes 8912896 | tf_op jit(solution)/shard_map/all_gather | solution.py:55
  254.8 156.0 %reduce-scatter.5.cloned.1.call-start = ((), (), s32[]{:S(2)}) async-start(), calls=%async_computation.7 | async-start | bytes 2228224 | tf_op jit(solution)/shard_map/reduce_scatter | solution.py:63
Sparse Core Ops, SparseCore 0:
  40.0 100.3 reduce-scatter.2
  255.0 55.0 all-gather.1
  321.0 89.8 reduce-scatter.4

commit v2 on v1

v2 whole, which is shorter than its diff:
```python
import jax
import jax.numpy as jnp
import numpy as np
from jax import lax
from jax.sharding import Mesh
from jax.sharding import PartitionSpec as P

scaling_divisor = 2.0
SEC = ("pair", "core")


def _lse(x, axes):
    top = jnp.max(x, axis=axes, keepdims=True)
    return top + jnp.log(jnp.sum(jnp.exp(x - top), axis=axes, keepdims=True))


def local(hidden, head, exit_loss_weight):
    pairs = lax.axis_size("pair")
    sections = pairs * 2
    tensors = lax.axis_size("tensor")
    _, tok, width = hidden.shape
    exits = sections
    dblk = width // sections
    vblk = head.shape[1]
    tps = tok // sections
    n_eq = tensors // tps
    kpe = exits // n_eq

    partner_head = lax.ppermute(head, "core", perm=[(0, 1), (1, 0)])
    head_pair = jnp.concatenate([head, partner_head], axis=0)

    h6 = hidden[0].reshape(pairs, 2, tps, pairs, 2, dblk)
    a = h6.transpose(3, 1, 0, 2, 4, 5)
    fwd = jnp.stack([a[:, 0], a[:, 1, :, :, ::-1, :]], axis=1)
    full = hidden[0].reshape(tok, sections, dblk).transpose(1, 0, 2)
    send = jnp.stack(
        [fwd.reshape(sections, -1), full.reshape(sections, -1)], axis=1
    )
    recv = lax.all_to_all(send, SEC, 0, 0, tiled=True)
    cols = recv[:, 1].reshape(exits, tok, dblk)
    lhs = recv[:, 0].reshape(exits, pairs, tps, 2 * dblk).transpose(1, 0, 2, 3)
    lhs = lhs.reshape(pairs * exits * tps, 2 * dblk)
    part = jnp.dot(lhs, head_pair, preferred_element_type=jnp.float32)
    part, w_local = lax.optimization_barrier((part, exit_loss_weight))
    weights = lax.all_gather(w_local, SEC, axis=0, tiled=True)
    own = lax.psum_scatter(part, "pair", scatter_dimension=0, tiled=True)
    own, weights = lax.optimization_barrier((own, weights))
    own = own.reshape(n_eq, kpe, tps, vblk)
    stud = own.transpose(2, 0, 1, 3).reshape(tensors, kpe, vblk)
    teach = jnp.broadcast_to(own[n_eq - 1, kpe - 1][:, None, None, :], (tps, n_eq, 1, vblk))
    send2 = jnp.concatenate([stud, teach.reshape(tensors, 1, vblk)], axis=1)
    rows = lax.all_to_all(send2, "tensor", 0, 0, tiled=True)

    logits = rows[:, :kpe, :]
    teacher = rows[:, kpe, :] / scaling_divisor
    log_student = logits - _lse(logits, (0, 2))
    log_teacher = teacher - _lse(teacher, (0, 1))
    log_mixture = jnp.logaddexp(log_student, log_teacher[:, None, :]) - jnp.log(2.0)
    halfgap = 0.5 * (log_student - log_mixture)
    student = jnp.exp(log_student)
    average = jnp.sum(student * halfgap, axis=(0, 2), keepdims=True)

    eq = lax.rem(lax.axis_index("tensor"), n_eq)
    wk = lax.dynamic_slice(weights, (eq * kpe,), (kpe,))
    grad_logits = (wk[None, :, None] * student * (halfgap - average)).astype(jnp.bfloat16)

    back = lax.all_to_all(grad_logits, "tensor", 0, 0, tiled=True)
    back = back.reshape(tps, exits, vblk)
    piece = lax.all_gather(back, SEC, axis=0, tiled=True)

    head_grad = lax.dot_general(
        cols, piece, (((0, 1), (1, 0)), ((), ())), preferred_element_type=jnp.float32
    )
    row_grad = lax.dot_general(
        piece, head, (((2,), (1,)), ((), ())), preferred_element_type=jnp.float32
    )
    grad_hidden = lax.psum_scatter(row_grad, "tensor", scatter_dimension=1, tiled=True)
    grad_hidden = grad_hidden.reshape(tok, dblk)
    return (grad_hidden, head_grad.astype(jnp.bfloat16))


def solution(mesh):
    shape = mesh.devices.shape
    inner = Mesh(
        np.asarray(mesh.devices).reshape(shape[0] // 2, 2, shape[1]), ("pair", "core", "tensor")
    )
    placed = (P(SEC, None, None), P(SEC, "tensor"), P(SEC))
    return jax.shard_map(
        local,
        mesh=inner,
        in_specs=placed,
        out_specs=(P("tensor", SEC), P(SEC, "tensor")),
        check_vma=False,
    )
```

time: 418 us -> 440 us (1.053); the launches traced: 417 us -> 433 us
  blocking collectives: 107 us -> 51.3 us
  waiting for transfers between devices: 229 us -> 259 us
  local copies, waits for them, and re-layouts: 17.2 us -> 33.6 us
  matrix products: 28.7 us -> 44.5 us
  starting transfers between devices: 9.89 us -> 16.5 us
    all_to_all x1 -> x2, waiting for transfers between devices: 0.01 us -> 78.3 us  [the longest x1 51.2 us: local(): rows = lax.all_to_all(send2, 'tensor', 0, 0, tiled=True)]
    unnamed x1 -> x0, blocking collectives: 65.7 us -> none
    reduce_scatter x1, waiting for transfers between devices: 101 us -> 65.4 us  [local(): own = lax.psum_scatter(part, 'pair', scatter_dimension=0, tiled=True)]
    optimization_barrier x0 -> x1, blocking collectives: none -> 29.3 us  [local(): own, weights = lax.optimization_barrier((own, weights))]
    all_to_all x1 -> x0, blocking collectives: 19.1 us -> none  [local(): cols = lax.all_to_all(x, 'section', 0, 0, tiled=True)]
    dot_general x1, matrix products: 10.3 us -> 25 us  [local(): lax.dot_general(cols, piece, (((0, 1), (1, 0)), ((), ())), preferred_elem...]
    slice x0 -> x2, local copies, waits for them, and re-layouts: none -> 11.7 us  [the longest x1 9.95 us: local(): cols = recv[:, 1].reshape(exits, tok, dblk)]
    another operation x0 -> x7, local copies, waits for them, and re-layouts: none -> 10.1 us  [the longest x3 4.84 us: local(): jnp.stack([fwd.reshape(sections, -1), full.reshape(sections, -1)], axis=1)]
  transfers between devices with their start and end apart: 4 -> 6, of which waited for: 3 -> 5; matrix products, arithmetic and copies ran while one was open for 4% -> 9% of each run, Pallas kernels for 0% -> 0%
where the time goes in v2:
time: 440 us; the launch traced here: 433 us
  waiting for transfers between devices  259 us (59%)
  blocking collectives  51.3 us (12%)
  matrix products  44.5 us (10%)
  local copies, waits for them, and re-layouts  33.6 us (8%)
  starting transfers between devices  16.5 us (4%)
  between operations  16.4 us (4%)
  other arithmetic  12 us (3%)
    reduce_scatter x1, waiting for transfers between devices, local(): own = lax.psum_scatter(part, 'pair', scatter_dimension=0, tiled=True)  65.4 us
    reduce_scatter x1, waiting for transfers between devices, local(): lax.psum_scatter(row_grad, 'tensor', scatter_dimension=1, tiled=True)  64.4 us
    all_to_all x1, waiting for transfers between devices, local(): rows = lax.all_to_all(send2, 'tensor', 0, 0, tiled=True)  51.2 us
    all_gather x1, waiting for transfers between devices, local(): piece = lax.all_gather(back, SEC, axis=0, tiled=True)  50.7 us
    optimization_barrier x1, blocking collectives, local(): own, weights = lax.optimization_barrier((own, weights))  29.3 us
    all_to_all x1, waiting for transfers between devices, local(): recv = lax.all_to_all(send, SEC, 0, 0, tiled=True)  27.1 us
    dot_general x1, matrix products, local(): lax.dot_general(cols, piece, (((0, 1), (1, 0)), ((), ())), preferred_elem...  25 us
    all_to_all x1, blocking collectives, local(): back = lax.all_to_all(grad_logits, 'tensor', 0, 0, tiled=True)  21.9 us
  transfers between devices with their start and end apart: 6, of which 5 were waited for; matrix products, arithmetic and copies ran while one was open for 9% of the time, Pallas kernels for 0%

profile of v2, /device:TPU:8, one launch (start us, length us, event | category | flops | bytes accessed | tf_op | source)
XLA Modules:
  0.0 433.2 jit_solution(12043793999282986412)
XLA Ops:
  7.2 1.8 reshape_squeeze.12
  9.0 1.0 copy.41
  10.0 1.8 fusion.12
  11.8 2.8 rev.3
  14.5 2.5 pad_maximum_fusion.2
  17.1 0.8 stack_reshape.6
  17.9 0.4 copy.31
  18.3 0.6 copy.40
  18.8 0.5 stack_reshape.7
  19.4 0.2 pad_maximum_fusion
  19.6 3.5 copy.25
  23.1 6.3 %all-to-all-start = ((bf16[16,2,32768]{2,1,0:T(2,128)(2,1)}), bf16[16,2,32768]{2,1,0:T(2,128)(2,1)S(1)}, u32[]{:S(2)}, u32[]{:S(2)}) async-start(bf16[16,2,32768]{2,1,0:T(2,128)(2,1)} %copy.25), calls=%async_computation | async-start | bytes 4194304 | tf_op jit(solution)/shard_map/all_to_all | solution.py:39
  29.4 0.4 collective-permute-start
  29.8 27.1 %all-to-all-done = bf16[16,2,32768]{2,1,0:T(2,128)(2,1)S(1)} async-done(((bf16[16,2,32768]{2,1,0:T(2,128)(2,1)}), bf16[16,2,32768]{2,1,0:T(2,128)(2,1)S(1)}, u32[]{:S(2)}, u32[]{:S(2)}) %all-to-all-start) | async-done | bytes 2097184 | tf_op jit(solution)/shard_map/all_to_all | solution.py:39
  56.9 10.0 %slice_reduce_fusion = (bf16[16,32768]{1,0:T(8,128)(2,1)S(1)}, bf16[16,32768]{1,0:T(8,128)(2,1)}) fusion(bf16[16,2,32768]{2,1,0:T(2,128)(2,1)S(1)} %all-to-all-done), kind=kLoop, calls=%fused_computation.9 | loop fusion | bytes 4194304 | tf_op jit(solution)/shard_map/slice | solution.py:40
  66.8 1.8 reshape_squeeze.14
  68.7 0.4 copy.26
  69.1 0.3 reshape.46
  69.4 11.2 %fusion = f32[512,4096]{1,0:T(8,128)} fusion(bf16[512,1024]{1,0:T(8,128)(2,1)S(1)} %reshape.46, bf16[512,4096]{1,0:T(8,128)(2,1)} %collective-permute-done, bf16[512,4096]{1,0:T(8,128)(2,1)} %param.4), kind=kOutput, calls=%fused_computation | convolution fusion | flops 4311744512 | bytes 17825792 | tf_op jit(solution)/shard_map/dot_general | solution.py:43
  81.3 0.6 dynamic-slice
  81.9 0.8 dynamic-update-slice
  82.6 29.3 %all-reduce = f32[16]{0:T(128)S(1)} all-reduce(f32[16]{0:T(128)S(1)} %dynamic-update-slice), channel_id=1, replica_groups=mesh['pair'=8,'core'=2,'tensor'=16] {'pair','core'}, use_global_device_ids=true, to_apply=%add | all-reduce | flops 16 | bytes 128 | tf_op jit(solution)/shard_map/optimization_barrier | solution.py:47
  112.0 65.4 %reduce-scatter.3.cloned.1.call-done = f32[64,4096]{1,0:T(8,128)} async-done(((f32[512,4096]{1,0:T(8,128)}), f32[64,4096]{1,0:T(8,128)}) %reduce-scatter.3.cloned.1.call-update) | async-done | bytes 1048592 | tf_op jit(solution)/shard_map/reduce_scatter | solution.py:46
  177.4 1.5 reshape.47
  179.0 0.7 copy.27
  179.7 0.4 broadcast_in_dim.8
  180.1 1.7 pad_maximum_fusion.1
  181.8 9.5 %all-to-all-start.1 = ((f32[16,5,4096]{2,1,0:T(8,128)}), f32[16,5,4096]{2,1,0:T(8,128)S(1)}, u32[]{:S(2)}, u32[]{:S(2)}) async-start(f32[16,5,4096]{2,1,0:T(8,128)} %pad_maximum_fusion.1), calls=%async_computation.2 | async-start | bytes 4194304 | tf_op jit(solution)/shard_map/all_to_all | solution.py:52
  191.3 0.3 all-gather.2.cloned.1.call-start
  191.6 0.1 dynamic_slice.3
  191.7 51.2 %all-to-all-done.1 = f32[16,5,4096]{2,1,0:T(8,128)S(1)} async-done(((f32[16,5,4096]{2,1,0:T(8,128)}), f32[16,5,4096]{2,1,0:T(8,128)S(1)}, u32[]{:S(2)}, u32[]{:S(2)}) %all-to-all-start.1) | async-done | bytes 1310752 | tf_op jit(solution)/shard_map/all_to_all | solution.py:52
  242.9 1.1 fusion.11
  244.1 1.8 exponential_reduce_fusion.1
  247.2 0.3 broadcast_subtract_fusion
  247.5 0.2 copy.42
  247.7 0.7 slice_reduce_fusion.2
  248.4 0.7 exponential_reduce_fusion
  249.1 2.2 multiply_reduce_fusion
  251.4 0.6 multiply_convert_fusion
  252.0 21.9 %all_to_all.15 = bf16[16,4,4096]{2,1,0:T(4,128)(2,1)S(1)} all-to-all(bf16[16,4,4096]{2,1,0:T(4,128)(2,1)S(1)} %multiply_convert_fusion), channel_id=1, replica_groups=mesh['pair'=8,'core'=2,'tensor'=16] {'tensor'}, dimensions={0} | all-to-all | bytes 1048576 | tf_op jit(solution)/shard_map/all_to_all | solution.py:67
  273.9 0.9 reshape.49
  274.8 0.0 reduce-scatter.5.cloned.1.call-start
  274.9 50.7 %all-gather.2.cloned.1.call-done = bf16[64,16,4096]{2,1,0:T(8,128)(2,1)} async-done(((bf16[4,16,4096]{2,1,0:T(8,128)(2,1)}), bf16[64,16,4096]{2,1,0:T(8,128)(2,1)}) %all-gather.2.cloned.1.call-update) | async-done | bytes 8388624 | tf_op jit(solution)/shard_map/all_gather | solution.py:69
  325.6 8.2 %fusion.8 = f32[64,16,512]{2,1,0:T(8,128)S(1)} fusion(bf16[64,16,4096]{2,1,0:T(8,128)(2,1)} %all-gather.2.cloned.1.call-done, bf16[512,4096]{1,0:T(8,128)(2,1)} %param.4), kind=kOutput, calls=%fused_computation.7 | convolution fusion | flops 4294967296 | bytes 14680064 | tf_op jit(solution)/shard_map/dot_general | solution.py:74
  333.8 2.6 copy.28
  336.5 0.3 copy.32
  336.8 25.0 %bitcast_convert_fusion = bf16[512,4096]{1,0:T(8,128)(2,1)} fusion(bf16[16,64,512]{2,1,0:T(8,128)(2,1)S(1)} %bitcast.38, bf16[64,16,4096]{2,1,0:T(8,128)(2,1)} %all-gather.2.cloned.1.call-done), kind=kOutput, calls=%fused_computation.4 | convolution fusion | flops 4297064448 | bytes 13631488 | tf_op jit(solution)/shard_map/dot_general | solution.py:71
  361.8 64.4 %reduce-scatter.5.cloned.1.call-done = f32[64,1,512]{2,0,1:T(8,128)} async-done(((f32[64,16,512]{2,0,1:T(8,128)}), f32[64,1,512]{2,0,1:T(8,128)}) %reduce-scatter.5.cloned.1.call-update) | async-done | bytes 131088 | tf_op jit(solution)/shard_map/reduce_scatter | solution.py:77
  (13 shorter events, 0.2 us)
Async XLA Ops:
  10.0 7.9 %copy-start = (bf16[1,64,8192]{2,1,0:T(8,128)(2,1)S(1)}, bf16[1,64,8192]{2,1,0:T(8,128)(2,1)}, u32[]{:S(2)}) copy-start(bf16[1,64,8192]{2,1,0:T(8,128)(2,1)} %param.3) | copy-start | bytes 3145732
  23.1 33.8 %all-to-all-start = ((bf16[16,2,32768]{2,1,0:T(2,128)(2,1)}), bf16[16,2,32768]{2,1,0:T(2,128)(2,1)S(1)}, u32[]{:S(2)}, u32[]{:S(2)}) async-start(bf16[16,2,32768]{2,1,0:T(2,128)(2,1)} %copy.25), calls=%async_computation | async-start | bytes 4194304 | tf_op jit(solution)/shard_map/all_to_all | solution.py:39
  29.4 148.1 %reduce-scatter.3.cloned.1.call-start = ((), (), s32[]{:S(2)}) async-start(), calls=%async_computation.5 | async-start | bytes 9437184 | tf_op jit(solution)/shard_map/reduce_scatter | solution.py:46
  29.4 40.0 %collective-permute-start = (bf16[512,4096]{1,0:T(8,128)(2,1)}, bf16[512,4096]{1,0:T(8,128)(2,1)}, u32[]{:S(2)}, u32[]{:S(2)}) collective-permute-start(bf16[512,4096]{1,0:T(8,128)(2,1)} %param.4), channel_id=1, source_target_pairs={{0,16},{16,0},{1,17},{17,1},{2,18},{18,2},{3,19},{19,3},{4,20},{20... | collective-permute-start | bytes 12582920 | tf_op jit(solution)/shard_map/ppermute | solution.py:29
  80.6 0.7 copy-start.1
  181.8 61.1 %all-to-all-start.1 = ((f32[16,5,4096]{2,1,0:T(8,128)}), f32[16,5,4096]{2,1,0:T(8,128)S(1)}, u32[]{:S(2)}, u32[]{:S(2)}) async-start(f32[16,5,4096]{2,1,0:T(8,128)} %pad_maximum_fusion.1), calls=%async_computation.2 | async-start | bytes 4194304 | tf_op jit(solution)/shard_map/all_to_all | solution.py:52
  191.3 134.3 %all-gather.2.cloned.1.call-start = ((), (), s32[]{:S(2)}) async-start(), calls=%async_computation.6 | async-start | bytes 8912896 | tf_op jit(solution)/shard_map/all_gather | solution.py:69
  274.8 151.4 %reduce-scatter.5.cloned.1.call-start = ((), (), s32[]{:S(2)}) async-start(), calls=%async_computation.7 | async-start | bytes 2228224 | tf_op jit(solution)/shard_map/reduce_scatter | solution.py:77
Sparse Core Ops, SparseCore 0:
  80.8 96.6 reduce-scatter.2
  275.0 50.6 all-gather.1
  336.6 89.5 reduce-scatter.4

commit v3 on v1

--- a/solution.py
+++ b/solution.py
@@ -29,7 +29,10 @@
     lhs = cols.reshape(exits, sections, tps, dblk).transpose(1, 0, 2, 3)
     lhs = lhs.reshape(sections * exits * tps, dblk)
     part = jnp.dot(lhs, head, preferred_element_type=jnp.float32)
+    part, w_local = lax.optimization_barrier((part, exit_loss_weight))
+    weights = lax.all_gather(w_local, "section", axis=0, tiled=True)
     own = lax.psum_scatter(part, "section", scatter_dimension=0, tiled=True)
+    own, weights = lax.optimization_barrier((own, weights))
     own = own.reshape(n_eq, kpe, tps, vblk)
     stud = own.transpose(2, 0, 1, 3).reshape(tensors, kpe, vblk)
     teach = jnp.broadcast_to(own[n_eq - 1, kpe - 1][:, None, None, :], (tps, n_eq, 1, vblk))
@@ -45,23 +48,22 @@
     student = jnp.exp(log_student)
     average = jnp.sum(student * halfgap, axis=(0, 2), keepdims=True)
 
-    weights = lax.all_gather(exit_loss_weight, "section", axis=0, tiled=True)
     eq = lax.rem(lax.axis_index("tensor"), n_eq)
     wk = lax.dynamic_slice(weights, (eq * kpe,), (kpe,))
     grad_logits = (wk[None, :, None] * student * (halfgap - average)).astype(jnp.bfloat16)
 
     back = lax.all_to_all(grad_logits, "tensor", 0, 0, tiled=True)
-    back = back.reshape(tps, exits, vblk)
-    piece = lax.all_gather(back, "section", axis=0, tiled=True)
+    back = back.reshape(tps, exits, vblk).transpose(1, 0, 2)
+    piece = lax.all_gather(back, "section", axis=1, tiled=True)
 
     head_grad = lax.dot_general(
-        cols, piece, (((0, 1), (1, 0)), ((), ())), preferred_element_type=jnp.float32
+        cols, piece, (((0, 1), (0, 1)), ((), ())), preferred_element_type=jnp.float32
     )
     row_grad = lax.dot_general(
         piece, head, (((2,), (1,)), ((), ())), preferred_element_type=jnp.float32
     )
-    grad_hidden = lax.psum_scatter(row_grad, "tensor", scatter_dimension=1, tiled=True)
-    grad_hidden = grad_hidden.reshape(tok, dblk)
+    parts = lax.all_to_all(row_grad, "tensor", 0, 0, tiled=True)
+    grad_hidden = jnp.sum(parts, axis=0)
     return (grad_hidden, head_grad.astype(jnp.bfloat16))
 
 

time: 418 us -> 374 us (0.89)
  blocking collectives: 107 us -> 68.2 us
  waiting for transfers between devices: 229 us -> 213 us
  starting transfers between devices: 9.89 us -> 19.4 us
    reduce_scatter x1 -> x0, waiting for transfers between devices: 73.4 us -> none  [local(): lax.psum_scatter(row_grad, 'tensor', scatter_dimension=1, tiled=True)]
    unnamed x1 -> x0, blocking collectives: 65.7 us -> none
    all_to_all x1, waiting for transfers between devices: 0.01 us -> 55.5 us  [local(): rows = lax.all_to_all(send, 'tensor', 0, 0, tiled=True)]
    all_to_all x0 -> x1, waiting for transfers between devices: none -> 37.3 us  [local(): parts = lax.all_to_all(row_grad, 'tensor', 0, 0, tiled=True)]
    reduce_scatter x1, waiting for transfers between devices: 101 us -> 71.3 us  [local(): own = lax.psum_scatter(part, 'section', scatter_dimension=0, tiled=True)]
    optimization_barrier x0 -> x1, blocking collectives: none -> 27.4 us  [local(): own, weights = lax.optimization_barrier((own, weights))]
    all_to_all x0 -> x1, starting transfers between devices: none -> 9.53 us  [local(): parts = lax.all_to_all(row_grad, 'tensor', 0, 0, tiled=True)]
    all_gather x1, waiting for transfers between devices: 55.2 us -> 49.3 us  [local(): piece = lax.all_gather(back, 'section', axis=1, tiled=True)]
  transfers between devices with their start and end apart: 4 -> 4, of which waited for: 3 -> 4; matrix products, arithmetic and copies ran while one was open for 4% -> 5% of each run, Pallas kernels for 0% -> 0%
where the time goes in v3:
time: 374 us; the launch traced here: 373 us
  waiting for transfers between devices  213 us (57%)
  blocking collectives  68.2 us (18%)
  matrix products  28.7 us (8%)
  starting transfers between devices  19.4 us (5%)
  local copies, waits for them, and re-layouts  17.2 us (5%)
  between operations  16.2 us (4%)
  other arithmetic  10.1 us (3%)
    reduce_scatter x1, waiting for transfers between devices, local(): own = lax.psum_scatter(part, 'section', scatter_dimension=0, tiled=True)  71.3 us
    all_to_all x1, waiting for transfers between devices, local(): rows = lax.all_to_all(send, 'tensor', 0, 0, tiled=True)  55.5 us
    all_gather x1, waiting for transfers between devices, local(): piece = lax.all_gather(back, 'section', axis=1, tiled=True)  49.3 us
    all_to_all x1, waiting for transfers between devices, local(): parts = lax.all_to_all(row_grad, 'tensor', 0, 0, tiled=True)  37.3 us
    optimization_barrier x1, blocking collectives, local(): own, weights = lax.optimization_barrier((own, weights))  27.4 us
    all_to_all x1, blocking collectives, local(): back = lax.all_to_all(grad_logits, 'tensor', 0, 0, tiled=True)  21.6 us
    all_to_all x1, blocking collectives, local(): cols = lax.all_to_all(x, 'section', 0, 0, tiled=True)  19.1 us
    dot_general x1, matrix products, local(): part = jnp.dot(lhs, head, preferred_element_type=jnp.float32)  10.3 us
  transfers between devices with their start and end apart: 4, of which 4 were waited for; matrix products, arithmetic and copies ran while one was open for 5% of the time, Pallas kernels for 0%

profile of v3, /device:TPU:8, one launch (start us, length us, event | category | flops | bytes accessed | tf_op | source)
XLA Modules:
  0.0 373.1 jit_solution(10065970637342622193)
XLA Ops:
  7.2 0.0 reduce-scatter.2.cloned.1.call-start
  7.2 1.6 copy.22
  8.8 0.6 copy.29
  9.4 19.1 %all_to_all.20 = bf16[16,64,512]{2,1,0:T(8,128)(2,1)S(1)} all-to-all(bf16[16,64,512]{2,1,0:T(8,128)(2,1)S(1)} %bitcast.33), channel_id=1, replica_groups=mesh['section'=16,'tensor'=16] {'section'}, dimensions={0} | all-to-all | bytes 2097152 | tf_op jit(solution)/shard_map/all_to_all | solution.py:28
  28.5 0.3 reshape.46
  28.8 0.5 copy.28
  29.3 0.3 reshape.47
  29.6 10.3 %fusion.5 = f32[1024,4096]{1,0:T(8,128)} fusion(bf16[1024,512]{1,0:T(8,128)(2,1)S(1)} %reshape.47, bf16[512,4096]{1,0:T(8,128)(2,1)} %param.4), kind=kOutput, calls=%fused_computation.21 | convolution fusion | flops 4294967296 | bytes 22020096 | tf_op jit(solution)/shard_map/dot_general | solution.py:31
  39.8 0.0 copy-start
  39.8 0.0 reduce-scatter.2.cloned.1.call-update
  40.5 0.0 copy-done
  40.5 0.6 dynamic-slice
  41.1 0.8 dynamic-update-slice
  41.9 27.4 %all-reduce = f32[16]{0:T(128)S(1)} all-reduce(f32[16]{0:T(128)S(1)} %dynamic-update-slice), channel_id=1, replica_groups=mesh['section'=16,'tensor'=16] {'section'}, use_global_device_ids=true, to_apply=%add | all-reduce | flops 16 | bytes 128 | tf_op jit(solution)/shard_map/optimization_barrier | solution.py:35
  69.3 71.3 %reduce-scatter.2.cloned.1.call-done = f32[64,4096]{1,0:T(8,128)} async-done(((f32[1024,4096]{1,0:T(8,128)}), f32[64,4096]{1,0:T(8,128)}) %reduce-scatter.2.cloned.1.call-update) | async-done | bytes 1048592 | tf_op jit(solution)/shard_map/reduce_scatter | solution.py:34
  140.6 1.5 reshape.48
  142.1 0.7 copy.13
  142.9 0.4 broadcast_in_dim.8
  143.2 1.7 pad_maximum_fusion
  145.0 9.8 %all-to-all-start.1 = ((f32[16,5,4096]{2,1,0:T(8,128)}), f32[16,5,4096]{2,1,0:T(8,128)S(1)}, u32[]{:S(2)}, u32[]{:S(2)}) async-start(f32[16,5,4096]{2,1,0:T(8,128)} %pad_maximum_fusion), calls=%async_computation.2 | async-start | bytes 4194304 | tf_op jit(solution)/shard_map/all_to_all | solution.py:40
  154.8 0.0 all-gather.2.cloned.1.call-start
  154.8 0.1 dynamic_slice.3
  154.9 55.5 %all-to-all-done.1 = f32[16,5,4096]{2,1,0:T(8,128)S(1)} async-done(((f32[16,5,4096]{2,1,0:T(8,128)}), f32[16,5,4096]{2,1,0:T(8,128)S(1)}, u32[]{:S(2)}, u32[]{:S(2)}) %all-to-all-start.1) | async-done | bytes 1310752 | tf_op jit(solution)/shard_map/all_to_all | solution.py:40
  210.4 1.1 fusion.4
  211.5 1.8 exponential_reduce_fusion.1
  214.6 0.3 broadcast_subtract_fusion
  215.0 0.2 copy.30
  215.2 0.7 slice_reduce_fusion
  215.8 0.7 exponential_reduce_fusion
  216.6 2.2 multiply_reduce_fusion
  218.8 0.6 multiply_convert_fusion
  219.4 21.6 %all_to_all.21 = bf16[16,4,4096]{2,1,0:T(4,128)(2,1)S(1)} all-to-all(bf16[16,4,4096]{2,1,0:T(4,128)(2,1)S(1)} %multiply_convert_fusion), channel_id=1, replica_groups=mesh['section'=16,'tensor'=16] {'tensor'}, dimensions={0} | all-to-all | bytes 1048576 | tf_op jit(solution)/shard_map/all_to_all | solution.py:55
  241.0 0.9 reshape.50
  242.0 0.0 all-gather.2.cloned.1.call-update
  242.0 49.3 %all-gather.2.cloned.1.call-done = bf16[16,64,4096]{2,0,1:T(8,128)(2,1)} async-done(((bf16[16,4,4096]{2,0,1:T(8,128)(2,1)}), bf16[16,64,4096]{2,0,1:T(8,128)(2,1)}) %all-gather.2.cloned.1.call-update) | async-done | bytes 8388624 | tf_op jit(solution)/shard_map/all_gather | solution.py:57
  291.3 8.2 %fusion.1 = f32[16,64,512]{2,0,1:T(8,128)S(1)} fusion(bf16[16,64,4096]{2,0,1:T(8,128)(2,1)} %all-gather.2.cloned.1.call-done, bf16[512,4096]{1,0:T(8,128)(2,1)} %param.4), kind=kOutput, calls=%fused_computation.2 | convolution fusion | flops 4294967296 | bytes 14680064 | tf_op jit(solution)/shard_map/dot_general | solution.py:62
  299.5 2.6 copy.18
  302.1 9.5 %all-to-all-start.3 = ((f32[16,64,512]{2,1,0:T(8,128)}), f32[16,64,512]{2,1,0:T(8,128)S(1)}, u32[]{:S(2)}, u32[]{:S(2)}) async-start(f32[16,64,512]{2,1,0:T(8,128)} %copy.18), calls=%async_computation.4 | async-start | bytes 4194304 | tf_op jit(solution)/shard_map/all_to_all | solution.py:65
  311.6 10.2 %fusion = bf16[512,4096]{0,1:T(8,128)(2,1)} fusion(bf16[16,64,4096]{2,0,1:T(8,128)(2,1)} %all-gather.2.cloned.1.call-done, bf16[16,64,512]{2,1,0:T(8,128)(2,1)S(1)} %all_to_all.20), kind=kOutput, calls=%fused_computation.1 | convolution fusion | flops 4297064448 | bytes 13631488 | tf_op jit(solution)/shard_map/dot_general | solution.py:59
  321.9 6.3 %copy.16 = bf16[512,4096]{1,0:T(8,128)(2,1)} copy(bf16[512,4096]{0,1:T(8,128)(2,1)} %fusion) | data formatting | bytes 8388608
  328.2 37.3 %all-to-all-done.3 = f32[16,64,512]{2,1,0:T(8,128)S(1)} async-done(((f32[16,64,512]{2,1,0:T(8,128)}), f32[16,64,512]{2,1,0:T(8,128)S(1)}, u32[]{:S(2)}, u32[]{:S(2)}) %all-to-all-start.3) | async-done | bytes 2097184 | tf_op jit(solution)/shard_map/all_to_all | solution.py:65
  365.4 0.8 reduce_sum.39
  (4 shorter events, 0.1 us)
Async XLA Ops:
  7.2 133.4 %reduce-scatter.2.cloned.1.call-start = ((), (), s32[]{:S(2)}) async-start(), calls=%async_computation.5 | async-start | bytes 17825792 | tf_op jit(solution)/shard_map/reduce_scatter | solution.py:34
  39.8 0.7 copy-start
  145.0 65.4 %all-to-all-start.1 = ((f32[16,5,4096]{2,1,0:T(8,128)}), f32[16,5,4096]{2,1,0:T(8,128)S(1)}, u32[]{:S(2)}, u32[]{:S(2)}) async-start(f32[16,5,4096]{2,1,0:T(8,128)} %pad_maximum_fusion), calls=%async_computation.2 | async-start | bytes 4194304 | tf_op jit(solution)/shard_map/all_to_all | solution.py:40
  154.8 136.5 %all-gather.2.cloned.1.call-start = ((), (), s32[]{:S(2)}) async-start(), calls=%async_computation.6 | async-start | bytes 8912896 | tf_op jit(solution)/shard_map/all_gather | solution.py:57
  302.1 63.4 %all-to-all-start.3 = ((f32[16,64,512]{2,1,0:T(8,128)}), f32[16,64,512]{2,1,0:T(8,128)S(1)}, u32[]{:S(2)}, u32[]{:S(2)}) async-start(f32[16,64,512]{2,1,0:T(8,128)} %copy.18), calls=%async_computation.4 | async-start | bytes 4194304 | tf_op jit(solution)/shard_map/all_to_all | solution.py:65
Sparse Core Ops, SparseCore 0:
  40.0 100.5 reduce-scatter.1
  242.1 49.1 all-gather.1

commit v4 on v3

v4 whole, which is shorter than its diff:
```python
import jax
import jax.numpy as jnp
from jax import lax
from jax.sharding import PartitionSpec as P

scaling_divisor = 2.0
NCHUNK = 2


def _lse(x, axes):
    top = jnp.max(x, axis=axes, keepdims=True)
    return top + jnp.log(jnp.sum(jnp.exp(x - top), axis=axes, keepdims=True))


def local(hidden, head, exit_loss_weight):
    sections = lax.axis_size("section")
    tensors = lax.axis_size("tensor")
    _, tok, width = hidden.shape
    exits = sections
    dblk = width // sections
    vblk = head.shape[1]
    tps = tok // sections
    tpc = tps // NCHUNK
    n_eq = tensors // tpc
    kpe = exits // n_eq

    x = hidden[0].reshape(tok, sections, dblk).transpose(1, 0, 2)
    cols = lax.all_to_all(x, "section", 0, 0, tiled=True)
    cols4 = cols.reshape(exits, sections, tps, dblk)

    eq = lax.rem(lax.axis_index("tensor"), n_eq)
    parts = []
    for c in range(NCHUNK):
        sub = cols4[:, :, c * tpc:(c + 1) * tpc, :]
        lhs = sub.transpose(1, 0, 2, 3).reshape(sections * exits * tpc, dblk)
        parts.append(jnp.dot(lhs, head, preferred_element_type=jnp.float32))
    first, w_local = lax.optimization_barrier((parts[0], exit_loss_weight))
    parts[0] = first
    weights = lax.all_gather(w_local, "section", axis=0, tiled=True)
    owns = [lax.psum_scatter(p, "section", scatter_dimension=0, tiled=True) for p in parts]
    owns[0], weights = lax.optimization_barrier((owns[0], weights))

    pieces = []
    prev = None
    for c in range(NCHUNK):
        own = owns[c]
        if prev is not None:
            own, prev = lax.optimization_barrier((own, prev))
        own = own.reshape(n_eq, kpe, tpc, vblk)
        stud = own.transpose(2, 0, 1, 3).reshape(tensors, kpe, vblk)
        teach = jnp.broadcast_to(own[n_eq - 1, kpe - 1][:, None, None, :], (tpc, n_eq, 1, vblk))
        send = jnp.concatenate([stud, teach.reshape(tensors, 1, vblk)], axis=1)
        rows = lax.all_to_all(send, "tensor", 0, 0, tiled=True)

        logits = rows[:, :kpe, :]
        teacher = rows[:, kpe, :] / scaling_divisor
        log_student = logits - _lse(logits, (0, 2))
        log_teacher = teacher - _lse(teacher, (0, 1))
        log_mixture = jnp.logaddexp(log_student, log_teacher[:, None, :]) - jnp.log(2.0)
        halfgap = 0.5 * (log_student - log_mixture)
        student = jnp.exp(log_student)
        average = jnp.sum(student * halfgap, axis=(0, 2), keepdims=True)
        wk = lax.dynamic_slice(weights, (eq * kpe,), (kpe,))
        grad_logits = (wk[None, :, None] * student * (halfgap - average)).astype(jnp.bfloat16)

        back = lax.all_to_all(grad_logits, "tensor", 0, 0, tiled=True)
        prev = back
        back = back.reshape(tpc, exits, vblk).transpose(1, 0, 2)
        pieces.append(lax.all_gather(back, "section", axis=1, tiled=True))

    head_grad = None
    row_grads = []
    for c in range(NCHUNK):
        piece = pieces[c]
        sub = cols4[:, :, c * tpc:(c + 1) * tpc, :].reshape(exits, sections * tpc, dblk)
        contrib = lax.dot_general(
            sub, piece, (((0, 1), (0, 1)), ((), ())), preferred_element_type=jnp.float32
        )
        head_grad = contrib if head_grad is None else head_grad + contrib
        row_grads.append(
            lax.dot_general(
                piece, head, (((2,), (1,)), ((), ())), preferred_element_type=jnp.float32
            ).reshape(exits, sections, tpc, dblk)
        )
    row_grad = jnp.stack(row_grads, axis=2).reshape(exits, tok, dblk)
    got = lax.all_to_all(row_grad, "tensor", 0, 0, tiled=True)
    grad_hidden = jnp.sum(got, axis=0)
    return (grad_hidden, head_grad.astype(jnp.bfloat16))


def solution(mesh):
    placed = (P("section", None, None), P("section", "tensor"), P("section"))
    return jax.shard_map(
        local,
        mesh=mesh,
        in_specs=placed,
        out_specs=(P("tensor", "section"), P("section", "tensor")),
        check_vma=False,
    )
```

time: 374 us -> 407 us (1.088)
  blocking collectives: 68.2 us -> 113 us
  waiting for transfers between devices: 213 us -> 187 us
  matrix products: 28.7 us -> 36.5 us
  local copies, waits for them, and re-layouts: 17.2 us -> 22.6 us
    all_to_all x0 -> x1, blocking collectives: none -> 35.6 us  [local(): rows = lax.all_to_all(send, 'tensor', 0, 0, tiled=True)]
    all_to_all x1, waiting for transfers between devices: 55.5 us -> 26.5 us  [local(): rows = lax.all_to_all(send, 'tensor', 0, 0, tiled=True)]
    all_to_all x1 -> x2, blocking collectives: 21.6 us -> 30.7 us  [local(): back = lax.all_to_all(grad_logits, 'tensor', 0, 0, tiled=True)]
    reduce_scatter x1 -> x2, waiting for transfers between devices: 71.3 us -> 76.5 us  [local(): lax.psum_scatter(p, 'section', scatter_dimension=0, tiled=True)]
    dot_general x2 -> x4, matrix products: 20.5 us -> 24.9 us  [the longest x2 15.5 us: local(): parts.append(jnp.dot(lhs, head, preferred_element_type=jnp.float32))]
    all_gather x1 -> x2, waiting for transfers between devices: 49.3 us -> 45.5 us  [local(): pieces.append(lax.all_gather(back, 'section', axis=1, tiled=True))]
    dot_general x1 -> x2, matrix products: 8.21 us -> 11.6 us  [local(): lax.dot_general(piece, head, (((2,), (1,)), ((), ())), preferred_element_...]
    unnamed x8 -> x11, local copies, waits for them, and re-layouts: 9.39 us -> 9.56 us
  transfers between devices with their start and end apart: 4 -> 6, of which waited for: 4 -> 5; matrix products, arithmetic and copies ran while one was open for 5% -> 13% of each run, Pallas kernels for 0% -> 0%
where the time goes in v4:
time: 407 us; the launch traced here: 406 us
  waiting for transfers between devices  187 us (46%)
  blocking collectives  113 us (28%)
  matrix products  36.5 us (9%)
  local copies, waits for them, and re-layouts  22.6 us (6%)
  between operations  17.4 us (4%)
  starting transfers between devices  17.2 us (4%)
  other arithmetic  12.6 us (3%)
    reduce_scatter x2, waiting for transfers between devices, local(): lax.psum_scatter(p, 'section', scatter_dimension=0, tiled=True)  76.5 us
    all_gather x2, waiting for transfers between devices, local(): pieces.append(lax.all_gather(back, 'section', axis=1, tiled=True))  45.5 us
    all_to_all x1, waiting for transfers between devices, local(): got = lax.all_to_all(row_grad, 'tensor', 0, 0, tiled=True)  38.2 us
    all_to_all x1, blocking collectives, local(): rows = lax.all_to_all(send, 'tensor', 0, 0, tiled=True)  35.6 us
    all_to_all x2, blocking collectives, local(): back = lax.all_to_all(grad_logits, 'tensor', 0, 0, tiled=True)  30.7 us
    optimization_barrier x1, blocking collectives, local(): owns[0], weights = lax.optimization_barrier((owns[0], weights))  27.4 us
    all_to_all x1, waiting for transfers between devices, local(): rows = lax.all_to_all(send, 'tensor', 0, 0, tiled=True)  26.5 us
    all_to_all x1, blocking collectives, local(): cols = lax.all_to_all(x, 'section', 0, 0, tiled=True)  19.1 us
  transfers between devices with their start and end apart: 6, of which 5 were waited for; matrix products, arithmetic and copies ran while one was open for 13% of the time, Pallas kernels for 0%

profile of v4, /device:TPU:8, one launch (start us, length us, event | category | flops | bytes accessed | tf_op | source)
XLA Modules:
  0.0 406.0 jit_solution(14665957189171574269)
XLA Ops:
  7.2 1.6 copy.82
  8.8 0.6 copy.60
  9.4 19.1 %all_to_all.30 = bf16[16,64,512]{2,1,0:T(8,128)(2,1)S(1)} all-to-all(bf16[16,64,512]{2,1,0:T(8,128)(2,1)S(1)} %copy.60), channel_id=1, replica_groups=mesh['section'=16,'tensor'=16] {'section'}, dimensions={0} | all-to-all | bytes 2097152 | tf_op jit(solution)/shard_map/all_to_all | solution.py:28
  28.5 0.6 copy.61
  29.3 0.5 copy.62
  30.1 7.7 %fusion.9 = f32[512,4096]{1,0:T(8,128)} fusion(bf16[512,512]{1,0:T(8,128)(2,1)S(1)} %reshape.94, bf16[512,4096]{1,0:T(8,128)(2,1)} %param.4), kind=kOutput, calls=%fused_computation.43 | convolution fusion | flops 2147483648 | bytes 13107200 | tf_op jit(solution)/shard_map/dot_general | solution.py:36
  37.9 0.5 copy.67
  38.6 7.8 %fusion.10 = f32[512,4096]{1,0:T(8,128)} fusion(bf16[512,512]{1,0:T(8,128)(2,1)S(1)} %reshape.98, bf16[512,4096]{1,0:T(8,128)(2,1)} %param.4), kind=kOutput, calls=%fused_computation.44 | convolution fusion | flops 2147483648 | bytes 13107200 | tf_op jit(solution)/shard_map/dot_general | solution.py:36
  47.1 0.6 dynamic-slice
  47.7 0.8 dynamic-update-slice
  48.4 27.4 %all-reduce = f32[16]{0:T(128)S(1)} all-reduce(f32[16]{0:T(128)S(1)} %dynamic-update-slice), channel_id=1, replica_groups=mesh['section'=16,'tensor'=16] {'section'}, use_global_device_ids=true, to_apply=%add | all-reduce | flops 16 | bytes 128 | tf_op jit(solution)/shard_map/optimization_barrier | solution.py:41
  75.9 38.1 %reduce-scatter.3.cloned.1.call-done = f32[32,4096]{1,0:T(8,128)} async-done(((f32[512,4096]{1,0:T(8,128)}), f32[32,4096]{1,0:T(8,128)}) %reduce-scatter.3.cloned.1.call-update) | async-done | bytes 524304 | tf_op jit(solution)/shard_map/reduce_scatter | solution.py:40
  114.0 1.3 reshape.95
  115.7 1.5 copy.64
  117.2 8.3 %all-to-all-start.1 = ((f32[16,3,4096]{2,1,0:T(4,128)}), f32[16,3,4096]{2,1,0:T(4,128)S(1)}, u32[]{:S(2)}, u32[]{:S(2)}) async-start(f32[16,3,4096]{2,1,0:T(4,128)} %copy.64), calls=%async_computation.2 | async-start | bytes 2097152 | tf_op jit(solution)/shard_map/all_to_all | solution.py:53
  125.8 26.5 %all-to-all-done.1 = f32[16,3,4096]{2,1,0:T(4,128)S(1)} async-done(((f32[16,3,4096]{2,1,0:T(4,128)}), f32[16,3,4096]{2,1,0:T(4,128)S(1)}, u32[]{:S(2)}, u32[]{:S(2)}) %all-to-all-start.1) | async-done | bytes 786464 | tf_op jit(solution)/shard_map/all_to_all | solution.py:53
  152.3 1.1 fusion.6
  153.5 1.8 exponential_reduce_fusion.3
  156.6 0.3 broadcast_subtract_fusion.1
  157.1 0.7 slice_reduce_fusion.1
  157.8 0.4 exponential_reduce_fusion.1
  158.2 0.7 multiply_reduce_fusion.1
  158.9 0.6 multiply_convert_fusion.1
  159.9 15.5 %all_to_all.31 = bf16[16,2,4096]{2,1,0:T(2,128)(2,1)S(1)} all-to-all(bf16[16,2,4096]{2,1,0:T(2,128)(2,1)S(1)} %copy.66), channel_id=1, replica_groups=mesh['section'=16,'tensor'=16] {'tensor'}, dimensions={0} | all-to-all | bytes 524288 | tf_op jit(solution)/shard_map/all_to_all | solution.py:66
  175.4 0.8 reshape.97
  176.2 38.4 %reduce-scatter.5.cloned.1.call-done = f32[32,4096]{1,0:T(8,128)} async-done(((f32[512,4096]{1,0:T(8,128)}), f32[32,4096]{1,0:T(8,128)}) %reduce-scatter.5.cloned.1.call-update) | async-done | bytes 524304 | tf_op jit(solution)/shard_map/reduce_scatter | solution.py:40
  214.7 1.3 reshape.99
  216.4 0.5 copy.69
  217.0 35.6 %all_to_all.32 = f32[16,3,4096]{2,1,0:T(4,128)S(1)} all-to-all(f32[16,3,4096]{2,1,0:T(4,128)S(1)} %copy.69), channel_id=1, replica_groups=mesh['section'=16,'tensor'=16] {'tensor'}, dimensions={0} | all-to-all | bytes 1572864 | tf_op jit(solution)/shard_map/all_to_all | solution.py:53
  252.5 1.1 fusion.7
  253.7 1.8 exponential_reduce_fusion.2
  256.8 0.3 broadcast_subtract_fusion
  257.3 0.7 slice_reduce_fusion
  258.0 0.4 exponential_reduce_fusion
  258.4 0.7 multiply_reduce_fusion
  259.1 0.6 multiply_convert_fusion
  260.1 15.2 %all_to_all.33 = bf16[16,2,4096]{2,1,0:T(2,128)(2,1)S(1)} all-to-all(bf16[16,2,4096]{2,1,0:T(2,128)(2,1)S(1)} %copy.71), channel_id=1, replica_groups=mesh['section'=16,'tensor'=16] {'tensor'}, dimensions={0} | all-to-all | bytes 524288 | tf_op jit(solution)/shard_map/all_to_all | solution.py:66
  275.3 0.8 reshape.101
  276.2 5.8 %fusion.4 = f32[16,32,512]{2,0,1:T(8,128)S(1)} fusion(bf16[16,32,4096]{2,0,1:T(8,128)(2,1)} %all-gather.3.cloned.1.call-done, bf16[512,4096]{1,0:T(8,128)(2,1)} %param.4), kind=kOutput, calls=%fused_computation.5 | convolution fusion | flops 2147483648 | bytes 9437184 | tf_op jit(solution)/shard_map/dot_general | solution.py:81
  282.0 45.5 %all-gather.5.cloned.1.call-done = bf16[16,32,4096]{2,0,1:T(8,128)(2,1)} async-done(((bf16[16,2,4096]{2,0,1:T(8,128)(2,1)}), bf16[16,32,4096]{2,0,1:T(8,128)(2,1)}) %all-gather.5.cloned.1.call-update) | async-done | bytes 4194320 | tf_op jit(solution)/shard_map/all_gather | solution.py:69
  327.5 5.8 %fusion.2 = f32[16,32,512]{2,0,1:T(8,128)S(1)} fusion(bf16[16,32,4096]{2,0,1:T(8,128)(2,1)} %all-gather.5.cloned.1.call-done, bf16[512,4096]{1,0:T(8,128)(2,1)} %param.4), kind=kOutput, calls=%fused_computation.3 | convolution fusion | flops 2147483648 | bytes 9437184 | tf_op jit(solution)/shard_map/dot_general | solution.py:81
  333.6 2.5 copy.74
  336.1 8.6 %all-to-all-start.5 = ((f32[16,64,512]{2,1,0:T(8,128)}), f32[16,64,512]{2,1,0:T(8,128)S(1)}, u32[]{:S(2)}, u32[]{:S(2)}) async-start(f32[16,64,512]{2,1,0:T(8,128)} %copy.74), calls=%async_computation.7 | async-start | bytes 4194304 | tf_op jit(solution)/shard_map/all_to_all | solution.py:86
  344.7 4.8 %fusion.11 = f32[4096,512,1]{1,0,2:T(8,128)S(1)} fusion(bf16[16,32,4096]{2,0,1:T(8,128)(2,1)} %all-gather.3.cloned.1.call-done, bf16[16,32,512]{2,0,1:T(8,128)(2,1)S(1)} %bitcast.88), kind=kOutput, calls=%fused_computation.45 | convolution fusion | flops 2147483648 | bytes 13107200 | tf_op jit(solution)/shard_map/dot_general | solution.py:76
  349.5 4.6 %fusion.1 = bf16[512,4096]{0,1:T(8,128)(2,1)} fusion(bf16[16,32,4096]{2,0,1:T(8,128)(2,1)S(1)} %copy-done, bf16[16,32,512]{2,0,1:T(8,128)(2,1)S(1)} %bitcast.87, f32[4096,512,1]{1,0,2:T(8,128)S(1)} %fusion.11), kind=kOutput, calls=%fused_computation.2 | convolution fusion | flops 2151677952 | bytes 17301504 | tf_op jit(solution)/shard_map/dot_general | solution.py:76
  354.1 6.3 %copy.75 = bf16[512,4096]{1,0:T(8,128)(2,1)} copy(bf16[512,4096]{0,1:T(8,128)(2,1)} %fusion.1) | data formatting | bytes 8388608
  360.4 38.2 %all-to-all-done.5 = f32[16,64,512]{2,1,0:T(8,128)S(1)} async-done(((f32[16,64,512]{2,1,0:T(8,128)}), f32[16,64,512]{2,1,0:T(8,128)S(1)}, u32[]{:S(2)}, u32[]{:S(2)}) %all-to-all-start.5) | async-done | bytes 2097184 | tf_op jit(solution)/shard_map/all_to_all | solution.py:86
  398.6 0.8 reduce_sum.69
  (33 shorter events, 3.0 us)
Async XLA Ops:
  7.2 106.8 %reduce-scatter.3.cloned.1.call-start = ((), (), s32[]{:S(2)}) async-start(), calls=%async_computation.8 | async-start | bytes 8912896 | tf_op jit(solution)/shard_map/reduce_scatter | solution.py:40
  37.8 176.8 %reduce-scatter.5.cloned.1.call-start = ((), (), s32[]{:S(2)}) async-start(), calls=%async_computation.10 | async-start | bytes 8912896 | tf_op jit(solution)/shard_map/reduce_scatter | solution.py:40
  46.4 0.7 copy-start.1
  117.2 35.1 %all-to-all-start.1 = ((f32[16,3,4096]{2,1,0:T(4,128)}), f32[16,3,4096]{2,1,0:T(4,128)S(1)}, u32[]{:S(2)}, u32[]{:S(2)}) async-start(f32[16,3,4096]{2,1,0:T(4,128)} %copy.64), calls=%async_computation.2 | async-start | bytes 2097152 | tf_op jit(solution)/shard_map/all_to_all | solution.py:53
  125.5 150.6 %all-gather.3.cloned.1.call-start = ((), (), s32[]{:S(2)}) async-start(), calls=%async_computation.9 | async-start | bytes 4456448 | tf_op jit(solution)/shard_map/all_gather | solution.py:69
  176.2 151.3 %all-gather.5.cloned.1.call-start = ((), (), s32[]{:S(2)}) async-start(), calls=%async_computation.11 | async-start | bytes 4456448 | tf_op jit(solution)/shard_map/all_gather | solution.py:69
  336.1 62.5 %all-to-all-start.5 = ((f32[16,64,512]{2,1,0:T(8,128)}), f32[16,64,512]{2,1,0:T(8,128)S(1)}, u32[]{:S(2)}, u32[]{:S(2)}) async-start(f32[16,64,512]{2,1,0:T(8,128)} %copy.74), calls=%async_computation.7 | async-start | bytes 4194304 | tf_op jit(solution)/shard_map/all_to_all | solution.py:86
  344.7 4.8 %copy-start = (bf16[16,32,4096]{2,0,1:T(8,128)(2,1)S(1)}, bf16[16,32,4096]{2,0,1:T(8,128)(2,1)}, u32[]{:S(2)}) copy-start(bf16[16,32,4096]{2,0,1:T(8,128)(2,1)} %all-gather.5.cloned.1.call-done) | copy-start | bytes 12582916
Sparse Core Ops, SparseCore 0:
  38.0 75.9 reduce-scatter.2
  116.5 98.1 reduce-scatter.4
  216.5 59.0 all-gather.2
  277.9 49.5 all-gather.4

commit v5 on v3

--- a/solution.py
+++ b/solution.py
@@ -62,8 +62,8 @@
     row_grad = lax.dot_general(
         piece, head, (((2,), (1,)), ((), ())), preferred_element_type=jnp.float32
     )
-    parts = lax.all_to_all(row_grad, "tensor", 0, 0, tiled=True)
-    grad_hidden = jnp.sum(parts, axis=0)
+    parts = lax.all_to_all(row_grad.astype(jnp.bfloat16), "tensor", 0, 0, tiled=True)
+    grad_hidden = jnp.sum(parts.astype(jnp.float32), axis=0)
     return (grad_hidden, head_grad.astype(jnp.bfloat16))
 
 

time: 374 us -> 350 us (0.936)
  waiting for transfers between devices: 213 us -> 190 us
    all_to_all x1, waiting for transfers between devices: 37.3 us -> 13.5 us  [local(): lax.all_to_all(row_grad.astype(jnp.bfloat16), 'tensor', 0, 0, tiled=True)]
where the time goes in v5:
time: 350 us; the launch traced here: 349 us
  waiting for transfers between devices  190 us (54%)
  blocking collectives  68.2 us (19%)
  matrix products  29.6 us (8%)
  starting transfers between devices  19.4 us (6%)
  local copies, waits for them, and re-layouts  16.2 us (5%)
  between operations  16.2 us (5%)
  other arithmetic  10.1 us (3%)
    reduce_scatter x1, waiting for transfers between devices, local(): own = lax.psum_scatter(part, 'section', scatter_dimension=0, tiled=True)  71.3 us
    all_to_all x1, waiting for transfers between devices, local(): rows = lax.all_to_all(send, 'tensor', 0, 0, tiled=True)  55.5 us
    all_gather x1, waiting for transfers between devices, local(): piece = lax.all_gather(back, 'section', axis=1, tiled=True)  49.3 us
    optimization_barrier x1, blocking collectives, local(): own, weights = lax.optimization_barrier((own, weights))  27.4 us
    all_to_all x1, blocking collectives, local(): back = lax.all_to_all(grad_logits, 'tensor', 0, 0, tiled=True)  21.6 us
    all_to_all x1, blocking collectives, local(): cols = lax.all_to_all(x, 'section', 0, 0, tiled=True)  19.1 us
    all_to_all x1, waiting for transfers between devices, local(): lax.all_to_all(row_grad.astype(jnp.bfloat16), 'tensor', 0, 0, tiled=True)  13.5 us
    dot_general x1, matrix products, local(): part = jnp.dot(lhs, head, preferred_element_type=jnp.float32)  10.3 us
  transfers between devices with their start and end apart: 4, of which 4 were waited for; matrix products, arithmetic and copies ran while one was open for 5% of the time, Pallas kernels for 0%

profile of v5, /device:TPU:8, one launch (start us, length us, event | category | flops | bytes accessed | tf_op | source)
XLA Modules:
  0.0 349.3 jit_solution(11056977310093579838)
XLA Ops:
  7.2 0.0 reduce-scatter.2.cloned.1.call-start
  7.2 1.6 copy.22
  8.8 0.6 copy.31
  9.4 19.1 %all_to_all.20 = bf16[16,64,512]{2,1,0:T(8,128)(2,1)S(1)} all-to-all(bf16[16,64,512]{2,1,0:T(8,128)(2,1)S(1)} %bitcast.33), channel_id=1, replica_groups=mesh['section'=16,'tensor'=16] {'section'}, dimensions={0} | all-to-all | bytes 2097152 | tf_op jit(solution)/shard_map/all_to_all | solution.py:28
  28.5 0.3 reshape.46
  28.8 0.5 copy.30
  29.3 0.3 reshape.47
  29.6 10.3 %fusion.5 = f32[1024,4096]{1,0:T(8,128)} fusion(bf16[1024,512]{1,0:T(8,128)(2,1)S(1)} %reshape.47, bf16[512,4096]{1,0:T(8,128)(2,1)} %param.4), kind=kOutput, calls=%fused_computation.23 | convolution fusion | flops 4294967296 | bytes 22020096 | tf_op jit(solution)/shard_map/dot_general | solution.py:31
  39.8 0.0 copy-start
  39.8 0.0 reduce-scatter.2.cloned.1.call-update
  40.5 0.0 copy-done
  40.5 0.6 dynamic-slice
  41.1 0.8 dynamic-update-slice
  41.9 27.4 %all-reduce = f32[16]{0:T(128)S(1)} all-reduce(f32[16]{0:T(128)S(1)} %dynamic-update-slice), channel_id=1, replica_groups=mesh['section'=16,'tensor'=16] {'section'}, use_global_device_ids=true, to_apply=%add | all-reduce | flops 16 | bytes 128 | tf_op jit(solution)/shard_map/optimization_barrier | solution.py:35
  69.3 71.3 %reduce-scatter.2.cloned.1.call-done = f32[64,4096]{1,0:T(8,128)} async-done(((f32[1024,4096]{1,0:T(8,128)}), f32[64,4096]{1,0:T(8,128)}) %reduce-scatter.2.cloned.1.call-update) | async-done | bytes 1048592 | tf_op jit(solution)/shard_map/reduce_scatter | solution.py:34
  140.6 1.5 reshape.48
  142.1 0.7 copy.13
  142.9 0.4 broadcast_in_dim.8
  143.2 1.7 pad_maximum_fusion
  145.0 9.8 %all-to-all-start.1 = ((f32[16,5,4096]{2,1,0:T(8,128)}), f32[16,5,4096]{2,1,0:T(8,128)S(1)}, u32[]{:S(2)}, u32[]{:S(2)}) async-start(f32[16,5,4096]{2,1,0:T(8,128)} %pad_maximum_fusion), calls=%async_computation.2 | async-start | bytes 4194304 | tf_op jit(solution)/shard_map/all_to_all | solution.py:40
  154.8 0.0 all-gather.2.cloned.1.call-start
  154.8 0.1 dynamic_slice.3
  154.9 55.5 %all-to-all-done.1 = f32[16,5,4096]{2,1,0:T(8,128)S(1)} async-done(((f32[16,5,4096]{2,1,0:T(8,128)}), f32[16,5,4096]{2,1,0:T(8,128)S(1)}, u32[]{:S(2)}, u32[]{:S(2)}) %all-to-all-start.1) | async-done | bytes 1310752 | tf_op jit(solution)/shard_map/all_to_all | solution.py:40
  210.4 1.1 fusion.4
  211.5 1.8 exponential_reduce_fusion.1
  214.6 0.3 broadcast_subtract_fusion
  215.0 0.2 copy.32
  215.2 0.7 slice_reduce_fusion
  215.8 0.7 exponential_reduce_fusion
  216.6 2.2 multiply_reduce_fusion
  218.8 0.6 multiply_convert_fusion
  219.4 21.6 %all_to_all.21 = bf16[16,4,4096]{2,1,0:T(4,128)(2,1)S(1)} all-to-all(bf16[16,4,4096]{2,1,0:T(4,128)(2,1)S(1)} %multiply_convert_fusion), channel_id=1, replica_groups=mesh['section'=16,'tensor'=16] {'tensor'}, dimensions={0} | all-to-all | bytes 1048576 | tf_op jit(solution)/shard_map/all_to_all | solution.py:55
  241.0 0.9 reshape.50
  242.0 0.0 all-gather.2.cloned.1.call-update
  242.0 49.3 %all-gather.2.cloned.1.call-done = bf16[16,64,4096]{2,0,1:T(8,128)(2,1)} async-done(((bf16[16,4,4096]{2,0,1:T(8,128)(2,1)}), bf16[16,64,4096]{2,0,1:T(8,128)(2,1)}) %all-gather.2.cloned.1.call-update) | async-done | bytes 8388624 | tf_op jit(solution)/shard_map/all_gather | solution.py:57
  291.3 9.1 %fusion.1 = bf16[16,64,512]{2,0,1:T(8,128)(2,1)S(1)} fusion(bf16[16,64,4096]{2,0,1:T(8,128)(2,1)} %all-gather.2.cloned.1.call-done, bf16[512,4096]{1,0:T(8,128)(2,1)} %param.4), kind=kOutput, calls=%fused_computation.2 | convolution fusion | flops 4294967296 | bytes 13631488 | tf_op jit(solution)/shard_map/dot_general | solution.py:62
  300.4 1.6 copy.29
  302.0 9.5 %all-to-all-start.3 = ((bf16[16,64,512]{2,1,0:T(8,128)(2,1)}), bf16[16,64,512]{2,1,0:T(8,128)(2,1)S(1)}, u32[]{:S(2)}, u32[]{:S(2)}) async-start(bf16[16,64,512]{2,1,0:T(8,128)(2,1)} %copy.29), calls=%async_computation.4 | async-start | bytes 2097152 | tf_op jit(solution)/shard_map/all_to_all | solution.py:65
  311.5 10.2 %fusion = bf16[512,4096]{0,1:T(8,128)(2,1)} fusion(bf16[16,64,4096]{2,0,1:T(8,128)(2,1)} %all-gather.2.cloned.1.call-done, bf16[16,64,512]{2,1,0:T(8,128)(2,1)S(1)} %all_to_all.20), kind=kOutput, calls=%fused_computation.1 | convolution fusion | flops 4297064448 | bytes 13631488 | tf_op jit(solution)/shard_map/dot_general | solution.py:59
  321.8 6.3 %copy.16 = bf16[512,4096]{1,0:T(8,128)(2,1)} copy(bf16[512,4096]{0,1:T(8,128)(2,1)} %fusion) | data formatting | bytes 8388608
  328.1 13.5 %all-to-all-done.3 = bf16[16,64,512]{2,1,0:T(8,128)(2,1)S(1)} async-done(((bf16[16,64,512]{2,1,0:T(8,128)(2,1)}), bf16[16,64,512]{2,1,0:T(8,128)(2,1)S(1)}, u32[]{:S(2)}, u32[]{:S(2)}) %all-to-all-start.3) | async-done | bytes 1048608 | tf_op jit(solution)/shard_map/all_to_all | solution.py:65
  341.6 0.8 convert_reduce_fusion
  (4 shorter events, 0.1 us)
Async XLA Ops:
  7.2 133.4 %reduce-scatter.2.cloned.1.call-start = ((), (), s32[]{:S(2)}) async-start(), calls=%async_computation.5 | async-start | bytes 17825792 | tf_op jit(solution)/shard_map/reduce_scatter | solution.py:34
  39.8 0.7 copy-start
  145.0 65.4 %all-to-all-start.1 = ((f32[16,5,4096]{2,1,0:T(8,128)}), f32[16,5,4096]{2,1,0:T(8,128)S(1)}, u32[]{:S(2)}, u32[]{:S(2)}) async-start(f32[16,5,4096]{2,1,0:T(8,128)} %pad_maximum_fusion), calls=%async_computation.2 | async-start | bytes 4194304 | tf_op jit(solution)/shard_map/all_to_all | solution.py:40
  154.8 136.5 %all-gather.2.cloned.1.call-start = ((), (), s32[]{:S(2)}) async-start(), calls=%async_computation.6 | async-start | bytes 8912896 | tf_op jit(solution)/shard_map/all_gather | solution.py:57
  302.0 39.6 %all-to-all-start.3 = ((bf16[16,64,512]{2,1,0:T(8,128)(2,1)}), bf16[16,64,512]{2,1,0:T(8,128)(2,1)S(1)}, u32[]{:S(2)}, u32[]{:S(2)}) async-start(bf16[16,64,512]{2,1,0:T(8,128)(2,1)} %copy.29), calls=%async_computation.4 | async-start | bytes 2097152 | tf_op jit(solution)/shard_map/all_to_all | solution.py:65
Sparse Core Ops, SparseCore 0:
  40.0 100.5 reduce-scatter.1
  242.1 49.1 all-gather.1

commit v6 on v5

v6 whole, which is shorter than its diff:
```python
import jax
import jax.numpy as jnp
from jax import lax
from jax.sharding import PartitionSpec as P

scaling_divisor = 2.0


def _gather_small(x, axis, count):
    sent = jnp.broadcast_to(x[None], (count,) + x.shape)
    return lax.all_to_all(sent, axis, 0, 0, tiled=True)


def local(hidden, head, exit_loss_weight):
    sections = lax.axis_size("section")
    tensors = lax.axis_size("tensor")
    _, tok, width = hidden.shape
    exits = sections
    dblk = width // sections
    vblk = head.shape[1]
    tps = tok // sections

    x = hidden[0].reshape(tok, sections, dblk).transpose(1, 0, 2)
    cols = lax.all_to_all(x, "section", 0, 0, tiled=True)
    lhs = cols.reshape(exits, sections, tps, dblk).transpose(1, 0, 2, 3)
    lhs = lhs.reshape(sections * exits * tps, dblk)
    part = jnp.dot(lhs, head, preferred_element_type=jnp.float32)
    part, w_local = lax.optimization_barrier((part, exit_loss_weight))
    weights = lax.all_gather(w_local, "section", axis=0, tiled=True)
    own = lax.psum_scatter(part, "section", scatter_dimension=0, tiled=True)
    own, weights = lax.optimization_barrier((own, weights))
    logits = own.reshape(exits, tps, vblk)
    teacher = logits[exits - 1] / scaling_divisor

    top_s = jnp.max(logits, axis=2)
    top_t = jnp.max(teacher, axis=1)
    sum_s = jnp.sum(jnp.exp(logits - top_s[:, :, None]), axis=2)
    sum_t = jnp.sum(jnp.exp(teacher - top_t[:, None]), axis=1)
    stats = jnp.stack(
        [jnp.concatenate([top_s.reshape(-1), top_t]), jnp.concatenate([sum_s.reshape(-1), sum_t])]
    )
    got = _gather_small(stats, "tensor", tensors)
    peak = jnp.max(got[:, 0], axis=0)
    norm = peak + jnp.log(jnp.sum(got[:, 1] * jnp.exp(got[:, 0] - peak[None]), axis=0))
    student_norm = norm[: exits * tps].reshape(exits, tps)
    teacher_norm = norm[exits * tps :]

    log_student = logits - student_norm[:, :, None]
    log_teacher = teacher - teacher_norm[:, None]
    log_mixture = jnp.logaddexp(log_student, log_teacher[None]) - jnp.log(2.0)
    halfgap = 0.5 * (log_student - log_mixture)
    student = jnp.exp(log_student)
    average = jnp.sum(_gather_small(jnp.sum(student * halfgap, axis=2), "tensor", tensors), axis=0)
    grad_logits = (
        weights[:, None, None] * student * (halfgap - average[:, :, None])
    ).astype(jnp.bfloat16)
    piece = lax.all_gather(grad_logits, "section", axis=1, tiled=True)

    head_grad = lax.dot_general(
        cols, piece, (((0, 1), (0, 1)), ((), ())), preferred_element_type=jnp.float32
    )
    row_grad = lax.dot_general(
        piece, head, (((2,), (1,)), ((), ())), preferred_element_type=jnp.float32
    )
    parts = lax.all_to_all(row_grad.astype(jnp.bfloat16), "tensor", 0, 0, tiled=True)
    grad_hidden = jnp.sum(parts.astype(jnp.float32), axis=0)
    return (grad_hidden, head_grad.astype(jnp.bfloat16))


def solution(mesh):
    placed = (P("section", None, None), P("section", "tensor"), P("section"))
    return jax.shard_map(
        local,
        mesh=mesh,
        in_specs=placed,
        out_specs=(P("tensor", "section"), P("section", "tensor")),
        check_vma=False,
    )
```

time: 350 us -> 295 us (0.84)
  waiting for transfers between devices: 190 us -> 144 us
  starting transfers between devices: 19.4 us -> 13.3 us
    all_to_all x1, waiting for transfers between devices: 55.5 us -> 9.23 us  [_gather_small(): return lax.all_to_all(sent, axis, 0, 0, tiled=True)]
    all_to_all x1, starting transfers between devices: 9.8 us -> 3.5 us  [_gather_small(): return lax.all_to_all(sent, axis, 0, 0, tiled=True)]
    unnamed x8 -> x9, local copies, waits for them, and re-layouts: 9.39 us -> 9.24 us
  transfers between devices with their start and end apart: 4 -> 4, of which waited for: 4 -> 4; matrix products, arithmetic and copies ran while one was open for 5% -> 6% of each run, Pallas kernels for 0% -> 0%
where the time goes in v6:
time: 295 us
  waiting for transfers between devices  144 us (49%)
  blocking collectives  66.1 us (22%)
  matrix products  29.6 us (10%)
  local copies, waits for them, and re-layouts  15.4 us (5%)
  between operations  14.8 us (5%)
  starting transfers between devices  13.3 us (5%)
  other arithmetic  11.5 us (4%)
    reduce_scatter x1, waiting for transfers between devices, local(): own = lax.psum_scatter(part, 'section', scatter_dimension=0, tiled=True)  71.3 us
    all_gather x1, waiting for transfers between devices, local(): piece = lax.all_gather(grad_logits, 'section', axis=1, tiled=True)  49.9 us
    optimization_barrier x1, blocking collectives, local(): own, weights = lax.optimization_barrier((own, weights))  27.4 us
    all_to_all x1, blocking collectives, _gather_small(): return lax.all_to_all(sent, axis, 0, 0, tiled=True)  19.6 us
    all_to_all x1, blocking collectives, local(): cols = lax.all_to_all(x, 'section', 0, 0, tiled=True)  19.1 us
    all_to_all x1, waiting for transfers between devices, local(): lax.all_to_all(row_grad.astype(jnp.bfloat16), 'tensor', 0, 0, tiled=True)  13.6 us
    dot_general x1, matrix products, local(): part = jnp.dot(lhs, head, preferred_element_type=jnp.float32)  10.3 us
    dot_general x1, matrix products, local(): lax.dot_general(cols, piece, (((0, 1), (0, 1)), ((), ())), preferred_elem...  10.2 us
  transfers between devices with their start and end apart: 4, of which 4 were waited for; matrix products, arithmetic and copies ran while one was open for 6% of the time, Pallas kernels for 0%

profile of v6, /device:TPU:8, one launch (start us, length us, event | category | flops | bytes accessed | tf_op | source)
XLA Modules:
  0.0 294.7 jit_solution(15544021231164241000)
XLA Ops:
  7.2 0.0 reduce-scatter.2.cloned.1.call-start
  7.2 1.6 copy.39
  8.8 0.6 copy.27
  9.4 19.1 %all_to_all.20 = bf16[16,64,512]{2,1,0:T(8,128)(2,1)S(1)} all-to-all(bf16[16,64,512]{2,1,0:T(8,128)(2,1)S(1)} %copy.27), channel_id=1, replica_groups=mesh['section'=16,'tensor'=16] {'section'}, dimensions={0} | all-to-all | bytes 2097152 | tf_op jit(solution)/shard_map/all_to_all | solution.py:24
  28.5 0.3 reshape.66
  28.8 0.5 copy.46
  29.3 0.3 reshape.67
  29.6 10.3 %fusion.10 = f32[1024,4096]{1,0:T(8,128)} fusion(bf16[1024,512]{1,0:T(8,128)(2,1)S(1)} %reshape.67, bf16[512,4096]{1,0:T(8,128)(2,1)} %param.4), kind=kOutput, calls=%fused_computation.22 | convolution fusion | flops 4294967296 | bytes 22020096 | tf_op jit(solution)/shard_map/dot_general | solution.py:27
  39.8 0.0 copy-start.1
  39.8 0.0 reduce-scatter.2.cloned.1.call-update
  40.5 0.0 copy-done.1
  40.5 0.6 dynamic-slice
  41.1 0.8 dynamic-update-slice
  41.9 27.4 %all-reduce = f32[16]{0:T(128)S(1)} all-reduce(f32[16]{0:T(128)S(1)} %dynamic-update-slice), channel_id=1, replica_groups=mesh['section'=16,'tensor'=16] {'section'}, use_global_device_ids=true, to_apply=%add | all-reduce | flops 16 | bytes 128 | tf_op jit(solution)/shard_map/optimization_barrier | solution.py:31
  69.3 71.3 %reduce-scatter.2.cloned.1.call-done = f32[64,4096]{1,0:T(8,128)} async-done(((f32[1024,4096]{1,0:T(8,128)}), f32[64,4096]{1,0:T(8,128)}) %reduce-scatter.2.cloned.1.call-update) | async-done | bytes 1048592 | tf_op jit(solution)/shard_map/reduce_scatter | solution.py:30
  140.6 0.0 copy-start
  140.6 1.1 fusion.8
  141.7 1.4 reduce_max.27
  143.1 1.5 exponential_reduce_fusion
  144.7 1.1 exponential_reduce_fusion.1
  145.8 0.1 maximum_bitcast_fusion
  145.9 19.6 %all_to_all.21 = f32[16,2,68]{2,1,0:T(2,128)S(1)} all-to-all(f32[16,2,68]{2,1,0:T(2,128)S(1)} %broadcast_in_dim.6), channel_id=1, replica_groups=mesh['section'=16,'tensor'=16] {'tensor'}, dimensions={0} | all-to-all | bytes 17408 | tf_op jit(solution)/shard_map/all_to_all | solution.py:11
  165.6 0.1 slice.23
  165.6 1.0 fusion.7
  166.6 0.2 sub.92.clone
  166.8 1.3 sub.98
  168.2 0.0 copy-done
  168.2 2.3 multiply_reduce_fusion
  170.5 0.1 broadcast_in_dim.7
  170.5 0.1 copy.33
  170.6 0.6 broadcast_in_dim.8
  171.3 3.5 %all-to-all-start.2 = ((f32[16,16,4]{1,2,0:T(4,128)}), f32[16,16,4]{1,2,0:T(4,128)S(1)}, u32[]{:S(2)}, u32[]{:S(2)}) async-start(f32[16,16,4]{1,2,0:T(4,128)} %broadcast_in_dim.8), calls=%async_computation.3 | async-start | bytes 65536 | tf_op jit(solution)/shard_map/all_to_all | solution.py:11
  174.8 0.2 all-gather.2.cloned.1.call-start
  175.0 0.3 reshape.68
  175.3 0.1 sub.87
  175.4 0.1 copy.30
  175.5 9.2 %all-to-all-done.2 = f32[16,16,4]{1,2,0:T(4,128)S(1)} async-done(((f32[16,16,4]{1,2,0:T(4,128)}), f32[16,16,4]{1,2,0:T(4,128)S(1)}, u32[]{:S(2)}, u32[]{:S(2)}) %all-to-all-start.2) | async-done | bytes 4128 | tf_op jit(solution)/shard_map/all_to_all | solution.py:11
  184.7 2.0 multiply_convert_fusion
  186.8 0.0 all-gather.2.cloned.1.call-update
  186.8 49.9 %all-gather.2.cloned.1.call-done = bf16[16,64,4096]{2,0,1:T(8,128)(2,1)} async-done(((bf16[16,4,4096]{2,0,1:T(8,128)(2,1)}), bf16[16,64,4096]{2,0,1:T(8,128)(2,1)}) %all-gather.2.cloned.1.call-update) | async-done | bytes 8388624 | tf_op jit(solution)/shard_map/all_gather | solution.py:57
  236.7 9.1 %fusion.3 = bf16[16,64,512]{2,0,1:T(8,128)(2,1)S(1)} fusion(bf16[16,64,4096]{2,0,1:T(8,128)(2,1)} %all-gather.2.cloned.1.call-done, bf16[512,4096]{1,0:T(8,128)(2,1)} %param.4), kind=kOutput, calls=%fused_computation.5 | convolution fusion | flops 4295491584 | bytes 13631488 | tf_op jit(solution)/shard_map/dot_general | solution.py:62
  245.8 1.6 copy.34
  247.5 9.5 %all-to-all-start.3 = ((bf16[16,64,512]{2,1,0:T(8,128)(2,1)}), bf16[16,64,512]{2,1,0:T(8,128)(2,1)S(1)}, u32[]{:S(2)}, u32[]{:S(2)}) async-start(bf16[16,64,512]{2,1,0:T(8,128)(2,1)} %copy.34), calls=%async_computation.4 | async-start | bytes 2097152 | tf_op jit(solution)/shard_map/all_to_all | solution.py:65
  257.0 10.2 %fusion = bf16[512,4096]{0,1:T(8,128)(2,1)} fusion(bf16[16,64,4096]{2,0,1:T(8,128)(2,1)} %all-gather.2.cloned.1.call-done, bf16[16,64,512]{2,1,0:T(8,128)(2,1)S(1)} %all_to_all.20), kind=kOutput, calls=%fused_computation.1 | convolution fusion | flops 4297064448 | bytes 13631488 | tf_op jit(solution)/shard_map/dot_general | solution.py:59
  267.2 6.3 %copy.36 = bf16[512,4096]{1,0:T(8,128)(2,1)} copy(bf16[512,4096]{0,1:T(8,128)(2,1)} %fusion) | data formatting | bytes 8388608
  273.6 13.6 %all-to-all-done.3 = bf16[16,64,512]{2,1,0:T(8,128)(2,1)S(1)} async-done(((bf16[16,64,512]{2,1,0:T(8,128)(2,1)}), bf16[16,64,512]{2,1,0:T(8,128)(2,1)S(1)}, u32[]{:S(2)}, u32[]{:S(2)}) %all-to-all-start.3) | async-done | bytes 1048608 | tf_op jit(solution)/shard_map/all_to_all | solution.py:65
  287.1 0.8 convert_reduce_fusion
  (8 shorter events, 0.1 us)
Async XLA Ops:
  7.2 133.4 %reduce-scatter.2.cloned.1.call-start = ((), (), s32[]{:S(2)}) async-start(), calls=%async_computation.5 | async-start | bytes 17825792 | tf_op jit(solution)/shard_map/reduce_scatter | solution.py:30
  39.8 0.7 copy-start.1
  140.6 27.6 %copy-start = (f32[64,4096]{1,0:T(8,128)S(1)}, f32[64,4096]{1,0:T(8,128)}, u32[]{:S(2)}) copy-start(f32[64,4096]{1,0:T(8,128)} %reduce-scatter.2.cloned.1.call-done) | copy-start | bytes 3145732
  171.3 13.4 %all-to-all-start.2 = ((f32[16,16,4]{1,2,0:T(4,128)}), f32[16,16,4]{1,2,0:T(4,128)S(1)}, u32[]{:S(2)}, u32[]{:S(2)}) async-start(f32[16,16,4]{1,2,0:T(4,128)} %broadcast_in_dim.8), calls=%async_computation.3 | async-start | bytes 65536 | tf_op jit(solution)/shard_map/all_to_all | solution.py:11
  174.8 62.0 %all-gather.2.cloned.1.call-start = ((), (), s32[]{:S(2)}) async-start(), calls=%async_computation.6 | async-start | bytes 8912896 | tf_op jit(solution)/shard_map/all_gather | solution.py:57
  247.5 39.6 %all-to-all-start.3 = ((bf16[16,64,512]{2,1,0:T(8,128)(2,1)}), bf16[16,64,512]{2,1,0:T(8,128)(2,1)S(1)}, u32[]{:S(2)}, u32[]{:S(2)}) async-start(bf16[16,64,512]{2,1,0:T(8,128)(2,1)} %copy.34), calls=%async_computation.4 | async-start | bytes 2097152 | tf_op jit(solution)/shard_map/all_to_all | solution.py:65
Sparse Core Ops, SparseCore 0:
  40.0 100.5 reduce-scatter.1
  186.9 49.7 all-gather.1

commit v7 on v6

--- a/solution.py
+++ b/solution.py
@@ -32,13 +32,10 @@
     logits = own.reshape(exits, tps, vblk)
     teacher = logits[exits - 1] / scaling_divisor
 
-    top_s = jnp.max(logits, axis=2)
-    top_t = jnp.max(teacher, axis=1)
-    sum_s = jnp.sum(jnp.exp(logits - top_s[:, :, None]), axis=2)
-    sum_t = jnp.sum(jnp.exp(teacher - top_t[:, None]), axis=1)
-    stats = jnp.stack(
-        [jnp.concatenate([top_s.reshape(-1), top_t]), jnp.concatenate([sum_s.reshape(-1), sum_t])]
-    )
+    rows = jnp.concatenate([own, teacher], axis=0)
+    top = jnp.max(rows, axis=1)
+    shifted = jnp.exp(rows - top[:, None])
+    stats = jnp.stack([top, jnp.sum(shifted, axis=1)])
     got = _gather_small(stats, "tensor", tensors)
     peak = jnp.max(got[:, 0], axis=0)
     norm = peak + jnp.log(jnp.sum(got[:, 1] * jnp.exp(got[:, 0] - peak[None]), axis=0))
@@ -49,7 +46,8 @@
     log_teacher = teacher - teacher_norm[:, None]
     log_mixture = jnp.logaddexp(log_student, log_teacher[None]) - jnp.log(2.0)
     halfgap = 0.5 * (log_student - log_mixture)
-    student = jnp.exp(log_student)
+    scale = jnp.exp(top - norm)[: exits * tps].reshape(exits, tps)
+    student = shifted[: exits * tps].reshape(exits, tps, vblk) * scale[:, :, None]
     average = jnp.sum(_gather_small(jnp.sum(student * halfgap, axis=2), "tensor", tensors), axis=0)
     grad_logits = (
         weights[:, None, None] * student * (halfgap - average[:, :, None])

time: 295 us -> 295 us (level)
    unnamed x9 -> x13, local copies, waits for them, and re-layouts: 9.24 us -> 9.25 us
where the time goes in v7:
time: 295 us; the launch traced here: 294 us
  waiting for transfers between devices  144 us (49%)
  blocking collectives  66.1 us (22%)
  matrix products  29.6 us (10%)
  local copies, waits for them, and re-layouts  15.9 us (5%)
  between operations  14.8 us (5%)
  starting transfers between devices  13.3 us (5%)
  other arithmetic  10.6 us (4%)
    reduce_scatter x1, waiting for transfers between devices, local(): own = lax.psum_scatter(part, 'section', scatter_dimension=0, tiled=True)  71.3 us
    all_gather x1, waiting for transfers between devices, local(): piece = lax.all_gather(grad_logits, 'section', axis=1, tiled=True)  49.9 us
    optimization_barrier x1, blocking collectives, local(): own, weights = lax.optimization_barrier((own, weights))  27.4 us
    all_to_all x1, blocking collectives, _gather_small(): return lax.all_to_all(sent, axis, 0, 0, tiled=True)  19.6 us
    all_to_all x1, blocking collectives, local(): cols = lax.all_to_all(x, 'section', 0, 0, tiled=True)  19.1 us
    all_to_all x1, waiting for transfers between devices, local(): lax.all_to_all(row_grad.astype(jnp.bfloat16), 'tensor', 0, 0, tiled=True)  13.5 us
    dot_general x1, matrix products, local(): part = jnp.dot(lhs, head, preferred_element_type=jnp.float32)  10.3 us
    dot_general x1, matrix products, local(): lax.dot_general(cols, piece, (((0, 1), (0, 1)), ((), ())), preferred_elem...  10.2 us
  transfers between devices with their start and end apart: 4, of which 4 were waited for; matrix products, arithmetic and copies ran while one was open for 6% of the time, Pallas kernels for 0%

profile of v7, /device:TPU:8, one launch (start us, length us, event | category | flops | bytes accessed | tf_op | source)
XLA Modules:
  0.0 293.9 jit_solution(13769614802653726558)
XLA Ops:
  7.2 0.0 reduce-scatter.2.cloned.1.call-start
  7.2 1.6 copy.45
  8.8 0.6 copy.31
  9.4 19.1 %all_to_all.20 = bf16[16,64,512]{2,1,0:T(8,128)(2,1)S(1)} all-to-all(bf16[16,64,512]{2,1,0:T(8,128)(2,1)S(1)} %copy.31), channel_id=1, replica_groups=mesh['section'=16,'tensor'=16] {'section'}, dimensions={0} | all-to-all | bytes 2097152 | tf_op jit(solution)/shard_map/all_to_all | solution.py:24
  28.5 0.3 reshape.88
  28.8 0.5 copy.59
  29.3 0.3 reshape.89
  29.6 10.3 %fusion.13 = f32[1024,4096]{1,0:T(8,128)} fusion(bf16[1024,512]{1,0:T(8,128)(2,1)S(1)} %reshape.89, bf16[512,4096]{1,0:T(8,128)(2,1)} %param.4), kind=kOutput, calls=%fused_computation.25 | convolution fusion | flops 4294967296 | bytes 22020096 | tf_op jit(solution)/shard_map/dot_general | solution.py:27
  39.8 0.0 copy-done.1
  39.8 0.0 reduce-scatter.2.cloned.1.call-update
  40.5 0.0 copy-done.3
  40.5 0.6 dynamic-slice
  41.1 0.8 dynamic-update-slice
  41.9 27.4 %all-reduce = f32[16]{0:T(128)S(1)} all-reduce(f32[16]{0:T(128)S(1)} %dynamic-update-slice), channel_id=1, replica_groups=mesh['section'=16,'tensor'=16] {'section'}, use_global_device_ids=true, to_apply=%add | all-reduce | flops 16 | bytes 128 | tf_op jit(solution)/shard_map/optimization_barrier | solution.py:31
  69.3 71.3 %reduce-scatter.2.cloned.1.call-done = f32[64,4096]{1,0:T(8,128)} async-done(((f32[1024,4096]{1,0:T(8,128)}), f32[64,4096]{1,0:T(8,128)}) %reduce-scatter.2.cloned.1.call-update) | async-done | bytes 1048592 | tf_op jit(solution)/shard_map/reduce_scatter | solution.py:30
  140.6 1.0 slice_multiply_fusion
  141.6 1.4 fusion.10
  143.0 1.6 fusion.11
  144.6 19.6 %all_to_all.21 = f32[16,2,68]{2,1,0:T(2,128)S(1)} all-to-all(f32[16,2,68]{2,1,0:T(2,128)S(1)} %broadcast_in_dim.6), channel_id=1, replica_groups=mesh['section'=16,'tensor'=16] {'tensor'}, dimensions={0} | all-to-all | bytes 17408 | tf_op jit(solution)/shard_map/all_to_all | solution.py:11
  164.3 0.1 slice.33
  164.3 1.0 broadcast_subtract_fusion
  165.3 0.2 sub.93.clone
  165.5 1.3 sub.99
  166.9 0.0 copy-done
  166.9 2.3 multiply_reduce_fusion
  169.2 0.1 broadcast_in_dim.7
  169.2 0.1 copy.39
  169.3 0.6 broadcast_in_dim.8
  170.0 3.5 %all-to-all-start.2 = ((f32[16,16,4]{1,2,0:T(4,128)}), f32[16,16,4]{1,2,0:T(4,128)S(1)}, u32[]{:S(2)}, u32[]{:S(2)}) async-start(f32[16,16,4]{1,2,0:T(4,128)} %broadcast_in_dim.8), calls=%async_computation.3 | async-start | bytes 65536 | tf_op jit(solution)/shard_map/all_to_all | solution.py:11
  173.5 0.2 all-gather.2.cloned.1.call-start
  173.7 0.3 reshape.91
  174.0 0.1 mul.46
  174.1 0.1 sub.88
  174.2 0.3 reshape.90
  174.5 0.1 copy.34
  174.6 0.1 copy.36
  174.7 8.7 %all-to-all-done.2 = f32[16,16,4]{1,2,0:T(4,128)S(1)} async-done(((f32[16,16,4]{1,2,0:T(4,128)}), f32[16,16,4]{1,2,0:T(4,128)S(1)}, u32[]{:S(2)}, u32[]{:S(2)}) %all-to-all-start.2) | async-done | bytes 4128 | tf_op jit(solution)/shard_map/all_to_all | solution.py:11
  183.4 2.5 fusion.9
  185.9 0.0 all-gather.2.cloned.1.call-update
  185.9 0.0 copy-start.2
  185.9 49.9 %all-gather.2.cloned.1.call-done = bf16[16,64,4096]{2,0,1:T(8,128)(2,1)} async-done(((bf16[16,4,4096]{2,0,1:T(8,128)(2,1)}), bf16[16,64,4096]{2,0,1:T(8,128)(2,1)}) %all-gather.2.cloned.1.call-update) | async-done | bytes 8388624 | tf_op jit(solution)/shard_map/all_gather | solution.py:55
  235.9 9.1 %fusion.3 = bf16[16,64,512]{2,0,1:T(8,128)(2,1)S(1)} fusion(bf16[16,64,4096]{2,0,1:T(8,128)(2,1)} %all-gather.2.cloned.1.call-done, bf16[512,4096]{1,0:T(8,128)(2,1)} %param.4), kind=kOutput, calls=%fused_computation.5 | convolution fusion | flops 4295491584 | bytes 13631488 | tf_op jit(solution)/shard_map/dot_general | solution.py:60
  245.0 1.6 copy.40
  246.6 9.5 %all-to-all-start.3 = ((bf16[16,64,512]{2,1,0:T(8,128)(2,1)}), bf16[16,64,512]{2,1,0:T(8,128)(2,1)S(1)}, u32[]{:S(2)}, u32[]{:S(2)}) async-start(bf16[16,64,512]{2,1,0:T(8,128)(2,1)} %copy.40), calls=%async_computation.4 | async-start | bytes 2097152 | tf_op jit(solution)/shard_map/all_to_all | solution.py:63
  256.1 10.2 %fusion = bf16[512,4096]{0,1:T(8,128)(2,1)} fusion(bf16[16,64,4096]{2,0,1:T(8,128)(2,1)} %all-gather.2.cloned.1.call-done, bf16[16,64,512]{2,1,0:T(8,128)(2,1)S(1)} %copy-done.2), kind=kOutput, calls=%fused_computation.1 | convolution fusion | flops 4297064448 | bytes 13631488 | tf_op jit(solution)/shard_map/dot_general | solution.py:57
  266.4 6.3 %copy.42 = bf16[512,4096]{1,0:T(8,128)(2,1)} copy(bf16[512,4096]{0,1:T(8,128)(2,1)} %fusion) | data formatting | bytes 8388608
  272.7 13.5 %all-to-all-done.3 = bf16[16,64,512]{2,1,0:T(8,128)(2,1)S(1)} async-done(((bf16[16,64,512]{2,1,0:T(8,128)(2,1)}), bf16[16,64,512]{2,1,0:T(8,128)(2,1)S(1)}, u32[]{:S(2)}, u32[]{:S(2)}) %all-to-all-start.3) | async-done | bytes 1048608 | tf_op jit(solution)/shard_map/all_to_all | solution.py:63
  286.2 0.8 convert_reduce_fusion
  (12 shorter events, 0.1 us)
Async XLA Ops:
  7.2 133.4 %reduce-scatter.2.cloned.1.call-start = ((), (), s32[]{:S(2)}) async-start(), calls=%async_computation.5 | async-start | bytes 17825792 | tf_op jit(solution)/shard_map/reduce_scatter | solution.py:30
  28.5 11.3 %copy-start.1 = (bf16[16,64,512]{2,1,0:T(8,128)(2,1)}, bf16[16,64,512]{2,1,0:T(8,128)(2,1)S(1)}, u32[]{:S(2)}) copy-start(bf16[16,64,512]{2,1,0:T(8,128)(2,1)S(1)} %all_to_all.20) | copy-start | bytes 3145732
  39.8 0.7 copy-start.3
  140.6 26.3 %copy-start = (f32[64,4096]{1,0:T(8,128)S(1)}, f32[64,4096]{1,0:T(8,128)}, u32[]{:S(2)}) copy-start(f32[64,4096]{1,0:T(8,128)} %reduce-scatter.2.cloned.1.call-done) | copy-start | bytes 3145732
  170.0 13.4 %all-to-all-start.2 = ((f32[16,16,4]{1,2,0:T(4,128)}), f32[16,16,4]{1,2,0:T(4,128)S(1)}, u32[]{:S(2)}, u32[]{:S(2)}) async-start(f32[16,16,4]{1,2,0:T(4,128)} %broadcast_in_dim.8), calls=%async_computation.3 | async-start | bytes 65536 | tf_op jit(solution)/shard_map/all_to_all | solution.py:11
  173.5 62.4 %all-gather.2.cloned.1.call-start = ((), (), s32[]{:S(2)}) async-start(), calls=%async_computation.6 | async-start | bytes 8912896 | tf_op jit(solution)/shard_map/all_gather | solution.py:55
  185.9 70.2 %copy-start.2 = (bf16[16,64,512]{2,1,0:T(8,128)(2,1)S(1)}, bf16[16,64,512]{2,1,0:T(8,128)(2,1)}, u32[]{:S(2)}) copy-start(bf16[16,64,512]{2,1,0:T(8,128)(2,1)} %copy-done.1) | copy-start | bytes 3145732
  246.6 39.6 %all-to-all-start.3 = ((bf16[16,64,512]{2,1,0:T(8,128)(2,1)}), bf16[16,64,512]{2,1,0:T(8,128)(2,1)S(1)}, u32[]{:S(2)}, u32[]{:S(2)}) async-start(bf16[16,64,512]{2,1,0:T(8,128)(2,1)} %copy.40), calls=%async_computation.4 | async-start | bytes 2097152 | tf_op jit(solution)/shard_map/all_to_all | solution.py:63
Sparse Core Ops, SparseCore 0:
  40.0 100.5 reduce-scatter.1
  186.1 49.7 all-gather.1

commit v8 on v7

--- a/solution.py
+++ b/solution.py
@@ -42,10 +42,9 @@
     student_norm = norm[: exits * tps].reshape(exits, tps)
     teacher_norm = norm[exits * tps :]
 
-    log_student = logits - student_norm[:, :, None]
-    log_teacher = teacher - teacher_norm[:, None]
-    log_mixture = jnp.logaddexp(log_student, log_teacher[None]) - jnp.log(2.0)
-    halfgap = 0.5 * (log_student - log_mixture)
+    gap = teacher[None] - logits
+    delta = teacher_norm[None, :] - student_norm
+    halfgap = 0.5 * jnp.log(2.0) - 0.5 * jax.nn.softplus(gap - delta[:, :, None])
     scale = jnp.exp(top - norm)[: exits * tps].reshape(exits, tps)
     student = shifted[: exits * tps].reshape(exits, tps, vblk) * scale[:, :, None]
     average = jnp.sum(_gather_small(jnp.sum(student * halfgap, axis=2), "tensor", tensors), axis=0)

time: 295 us -> 293 us (level)
  blocking collectives: 66.1 us -> 46.6 us
  starting transfers between devices: 13.3 us -> 23.1 us
  waiting for transfers between devices: 144 us -> 150 us
  local copies, waits for them, and re-layouts: 15.9 us -> 19 us
    all_to_all x1 -> x0, blocking collectives: 19.6 us -> none  [_gather_small(): return lax.all_to_all(sent, axis, 0, 0, tiled=True)]
    all_to_all x1 -> x2, starting transfers between devices: 3.5 us -> 13.3 us  [_gather_small(): return lax.all_to_all(sent, axis, 0, 0, tiled=True)]
    all_to_all x1 -> x2, waiting for transfers between devices: 8.75 us -> 14.8 us  [_gather_small(): return lax.all_to_all(sent, axis, 0, 0, tiled=True)]
  transfers between devices with their start and end apart: 4 -> 5, of which waited for: 4 -> 5; matrix products, arithmetic and copies ran while one was open for 6% -> 8% of each run, Pallas kernels for 0% -> 0%
where the time goes in v8:
time: 293 us; the launch traced here: 292 us
  waiting for transfers between devices  150 us (51%)
  blocking collectives  46.6 us (16%)
  matrix products  29.6 us (10%)
  starting transfers between devices  23.1 us (8%)
  local copies, waits for them, and re-layouts  19 us (6%)
  between operations  14.8 us (5%)
  other arithmetic  9.18 us (3%)
    reduce_scatter x1, waiting for transfers between devices, local(): own = lax.psum_scatter(part, 'section', scatter_dimension=0, tiled=True)  71.3 us
    all_gather x1, waiting for transfers between devices, local(): piece = lax.all_gather(grad_logits, 'section', axis=1, tiled=True)  49.9 us
    optimization_barrier x1, blocking collectives, local(): own, weights = lax.optimization_barrier((own, weights))  27.4 us
    all_to_all x1, blocking collectives, local(): cols = lax.all_to_all(x, 'section', 0, 0, tiled=True)  19.1 us
    all_to_all x2, waiting for transfers between devices, _gather_small(): return lax.all_to_all(sent, axis, 0, 0, tiled=True)  14.8 us
    all_to_all x1, waiting for transfers between devices, local(): lax.all_to_all(row_grad.astype(jnp.bfloat16), 'tensor', 0, 0, tiled=True)  13.5 us
    all_to_all x2, starting transfers between devices, _gather_small(): return lax.all_to_all(sent, axis, 0, 0, tiled=True)  13.3 us
    dot_general x1, matrix products, local(): part = jnp.dot(lhs, head, preferred_element_type=jnp.float32)  10.3 us
  transfers between devices with their start and end apart: 5, of which 5 were waited for; matrix products, arithmetic and copies ran while one was open for 8% of the time, Pallas kernels for 0%

profile of v8, /device:TPU:8, one launch (start us, length us, event | category | flops | bytes accessed | tf_op | source)
XLA Modules:
  0.0 291.9 jit_solution(18277966905644496205)
XLA Ops:
  7.2 0.0 reduce-scatter.2.cloned.1.call-start
  7.2 1.6 copy.46
  8.8 0.6 copy.31
  9.4 19.1 %all_to_all.20 = bf16[16,64,512]{2,1,0:T(8,128)(2,1)S(1)} all-to-all(bf16[16,64,512]{2,1,0:T(8,128)(2,1)S(1)} %copy.31), channel_id=1, replica_groups=mesh['section'=16,'tensor'=16] {'section'}, dimensions={0} | all-to-all | bytes 2097152 | tf_op jit(solution)/shard_map/all_to_all | solution.py:24
  28.5 0.3 reshape.81
  28.8 0.5 copy.60
  29.3 0.3 reshape.82
  29.6 10.3 %fusion.21 = f32[1024,4096]{1,0:T(8,128)} fusion(bf16[1024,512]{1,0:T(8,128)(2,1)S(1)} %reshape.82, bf16[512,4096]{1,0:T(8,128)(2,1)} %param.4), kind=kOutput, calls=%fused_computation.34 | convolution fusion | flops 4294967296 | bytes 22020096 | tf_op jit(solution)/shard_map/dot_general | solution.py:27
  39.8 0.0 copy-done.1
  39.8 0.0 reduce-scatter.2.cloned.1.call-update
  40.5 0.0 copy-done.3
  40.5 0.6 dynamic-slice
  41.1 0.8 dynamic-update-slice
  41.9 27.4 %all-reduce = f32[16]{0:T(128)S(1)} all-reduce(f32[16]{0:T(128)S(1)} %dynamic-update-slice), channel_id=1, replica_groups=mesh['section'=16,'tensor'=16] {'section'}, use_global_device_ids=true, to_apply=%add | all-reduce | flops 16 | bytes 128 | tf_op jit(solution)/shard_map/optimization_barrier | solution.py:31
  69.3 71.3 %reduce-scatter.2.cloned.1.call-done = f32[64,4096]{1,0:T(8,128)} async-done(((f32[1024,4096]{1,0:T(8,128)}), f32[64,4096]{1,0:T(8,128)}) %reduce-scatter.2.cloned.1.call-update) | async-done | bytes 1048592 | tf_op jit(solution)/shard_map/reduce_scatter | solution.py:30
  140.6 1.0 slice_multiply_fusion
  141.6 1.4 fusion.18
  143.0 1.6 fusion.19
  144.6 0.6 broadcast_in_dim.6
  145.2 9.8 %all-to-all-start.1 = ((f32[16,2,68]{2,1,0:T(2,128)}), f32[16,2,68]{2,1,0:T(2,128)S(1)}, u32[]{:S(2)}, u32[]{:S(2)}) async-start(f32[16,2,68]{2,1,0:T(2,128)} %broadcast_in_dim.6), calls=%async_computation.2 | async-start | bytes 32768 | tf_op jit(solution)/shard_map/all_to_all | solution.py:11
  155.0 1.2 sub.88.clone
  156.2 1.6 sub.96
  157.8 7.2 %all-to-all-done.1 = f32[16,2,68]{2,1,0:T(2,128)S(1)} async-done(((f32[16,2,68]{2,1,0:T(2,128)}), f32[16,2,68]{2,1,0:T(2,128)S(1)}, u32[]{:S(2)}, u32[]{:S(2)}) %all-to-all-start.1) | async-done | bytes 8736 | tf_op jit(solution)/shard_map/all_to_all | solution.py:11
  165.1 0.1 slice.34
  165.1 0.1 slice.36
  165.2 0.1 sub.98
  165.3 1.9 fusion.14
  167.2 0.1 broadcast_in_dim.7
  167.3 0.1 copy.39
  167.4 0.6 broadcast_in_dim.8
  168.0 3.5 %all-to-all-start.2 = ((f32[16,16,4]{1,2,0:T(4,128)}), f32[16,16,4]{1,2,0:T(4,128)S(1)}, u32[]{:S(2)}, u32[]{:S(2)}) async-start(f32[16,16,4]{1,2,0:T(4,128)} %broadcast_in_dim.8), calls=%async_computation.3 | async-start | bytes 65536 | tf_op jit(solution)/shard_map/all_to_all | solution.py:11
  171.5 0.2 all-gather.2.cloned.1.call-start
  171.7 0.3 reshape.84
  172.1 0.1 copy.37
  172.1 0.1 mul.46
  172.2 1.5 reshape.83
  173.8 0.1 copy.34
  173.8 7.6 %all-to-all-done.2 = f32[16,16,4]{1,2,0:T(4,128)S(1)} async-done(((f32[16,16,4]{1,2,0:T(4,128)}), f32[16,16,4]{1,2,0:T(4,128)S(1)}, u32[]{:S(2)}, u32[]{:S(2)}) %all-to-all-start.2) | async-done | bytes 4128 | tf_op jit(solution)/shard_map/all_to_all | solution.py:11
  181.5 2.5 fusion.10
  183.9 0.0 all-gather.2.cloned.1.call-update
  184.0 49.9 %all-gather.2.cloned.1.call-done = bf16[16,64,4096]{2,0,1:T(8,128)(2,1)} async-done(((bf16[16,4,4096]{2,0,1:T(8,128)(2,1)}), bf16[16,64,4096]{2,0,1:T(8,128)(2,1)}) %all-gather.2.cloned.1.call-update) | async-done | bytes 8388624 | tf_op jit(solution)/shard_map/all_gather | solution.py:54
  233.9 9.1 %fusion.3 = bf16[16,64,512]{2,0,1:T(8,128)(2,1)S(1)} fusion(bf16[16,64,4096]{2,0,1:T(8,128)(2,1)} %all-gather.2.cloned.1.call-done, bf16[512,4096]{1,0:T(8,128)(2,1)} %param.4), kind=kOutput, calls=%fused_computation.7 | convolution fusion | flops 4295491584 | bytes 13631488 | tf_op jit(solution)/shard_map/dot_general | solution.py:59
  243.0 1.6 copy.40
  244.6 9.5 %all-to-all-start.3 = ((bf16[16,64,512]{2,1,0:T(8,128)(2,1)}), bf16[16,64,512]{2,1,0:T(8,128)(2,1)S(1)}, u32[]{:S(2)}, u32[]{:S(2)}) async-start(bf16[16,64,512]{2,1,0:T(8,128)(2,1)} %copy.40), calls=%async_computation.4 | async-start | bytes 2097152 | tf_op jit(solution)/shard_map/all_to_all | solution.py:62
  254.2 10.2 %fusion = bf16[512,4096]{0,1:T(8,128)(2,1)} fusion(bf16[16,64,4096]{2,0,1:T(8,128)(2,1)} %all-gather.2.cloned.1.call-done, bf16[16,64,512]{2,1,0:T(8,128)(2,1)S(1)} %copy-done.2), kind=kOutput, calls=%fused_computation.1 | convolution fusion | flops 4297064448 | bytes 13631488 | tf_op jit(solution)/shard_map/dot_general | solution.py:56
  264.4 6.3 %copy.42 = bf16[512,4096]{1,0:T(8,128)(2,1)} copy(bf16[512,4096]{0,1:T(8,128)(2,1)} %fusion) | data formatting | bytes 8388608
  270.7 13.5 %all-to-all-done.3 = bf16[16,64,512]{2,1,0:T(8,128)(2,1)S(1)} async-done(((bf16[16,64,512]{2,1,0:T(8,128)(2,1)}), bf16[16,64,512]{2,1,0:T(8,128)(2,1)S(1)}, u32[]{:S(2)}, u32[]{:S(2)}) %all-to-all-start.3) | async-done | bytes 1048608 | tf_op jit(solution)/shard_map/all_to_all | solution.py:62
  284.3 0.8 convert_reduce_fusion
  (14 shorter events, 0.1 us)
Async XLA Ops:
  7.2 133.4 %reduce-scatter.2.cloned.1.call-start = ((), (), s32[]{:S(2)}) async-start(), calls=%async_computation.5 | async-start | bytes 17825792 | tf_op jit(solution)/shard_map/reduce_scatter | solution.py:30
  28.5 11.3 %copy-start.1 = (bf16[16,64,512]{2,1,0:T(8,128)(2,1)}, bf16[16,64,512]{2,1,0:T(8,128)(2,1)S(1)}, u32[]{:S(2)}) copy-start(bf16[16,64,512]{2,1,0:T(8,128)(2,1)S(1)} %all_to_all.20) | copy-start | bytes 3145732
  39.8 0.7 copy-start.3
  140.6 24.7 %copy-start = (f32[64,4096]{1,0:T(8,128)S(1)}, f32[64,4096]{1,0:T(8,128)}, u32[]{:S(2)}) copy-start(f32[64,4096]{1,0:T(8,128)} %reduce-scatter.2.cloned.1.call-done) | copy-start | bytes 3145732
  145.2 19.8 %all-to-all-start.1 = ((f32[16,2,68]{2,1,0:T(2,128)}), f32[16,2,68]{2,1,0:T(2,128)S(1)}, u32[]{:S(2)}, u32[]{:S(2)}) async-start(f32[16,2,68]{2,1,0:T(2,128)} %broadcast_in_dim.6), calls=%async_computation.2 | async-start | bytes 32768 | tf_op jit(solution)/shard_map/all_to_all | solution.py:11
  168.0 13.4 %all-to-all-start.2 = ((f32[16,16,4]{1,2,0:T(4,128)}), f32[16,16,4]{1,2,0:T(4,128)S(1)}, u32[]{:S(2)}, u32[]{:S(2)}) async-start(f32[16,16,4]{1,2,0:T(4,128)} %broadcast_in_dim.8), calls=%async_computation.3 | async-start | bytes 65536 | tf_op jit(solution)/shard_map/all_to_all | solution.py:11
  171.5 62.4 %all-gather.2.cloned.1.call-start = ((), (), s32[]{:S(2)}) async-start(), calls=%async_computation.6 | async-start | bytes 8912896 | tf_op jit(solution)/shard_map/all_gather | solution.py:54
  243.0 11.2 %copy-start.2 = (bf16[16,64,512]{2,1,0:T(8,128)(2,1)S(1)}, bf16[16,64,512]{2,1,0:T(8,128)(2,1)}, u32[]{:S(2)}) copy-start(bf16[16,64,512]{2,1,0:T(8,128)(2,1)} %copy-done.1) | copy-start | bytes 3145732
  244.6 39.6 %all-to-all-start.3 = ((bf16[16,64,512]{2,1,0:T(8,128)(2,1)}), bf16[16,64,512]{2,1,0:T(8,128)(2,1)S(1)}, u32[]{:S(2)}, u32[]{:S(2)}) async-start(bf16[16,64,512]{2,1,0:T(8,128)(2,1)} %copy.40), calls=%async_computation.4 | async-start | bytes 2097152 | tf_op jit(solution)/shard_map/all_to_all | solution.py:62
Sparse Core Ops, SparseCore 0:
  40.0 100.5 reduce-scatter.1
  184.1 49.7 all-gather.1

commit v9 on v8

--- a/solution.py
+++ b/solution.py
@@ -32,10 +32,12 @@
     logits = own.reshape(exits, tps, vblk)
     teacher = logits[exits - 1] / scaling_divisor
 
-    rows = jnp.concatenate([own, teacher], axis=0)
-    top = jnp.max(rows, axis=1)
-    shifted = jnp.exp(rows - top[:, None])
-    stats = jnp.stack([top, jnp.sum(shifted, axis=1)])
+    top_s = jnp.max(own, axis=1)
+    top_t = top_s[(exits - 1) * tps:] / scaling_divisor
+    shifted = jnp.exp(own - top_s[:, None])
+    sum_t = jnp.sum(jnp.exp(teacher - top_t[:, None]), axis=1)
+    top = jnp.concatenate([top_s, top_t])
+    stats = jnp.stack([top, jnp.concatenate([jnp.sum(shifted, axis=1), sum_t])])
     got = _gather_small(stats, "tensor", tensors)
     peak = jnp.max(got[:, 0], axis=0)
     norm = peak + jnp.log(jnp.sum(got[:, 1] * jnp.exp(got[:, 0] - peak[None]), axis=0))
@@ -46,7 +48,7 @@
     delta = teacher_norm[None, :] - student_norm
     halfgap = 0.5 * jnp.log(2.0) - 0.5 * jax.nn.softplus(gap - delta[:, :, None])
     scale = jnp.exp(top - norm)[: exits * tps].reshape(exits, tps)
-    student = shifted[: exits * tps].reshape(exits, tps, vblk) * scale[:, :, None]
+    student = shifted.reshape(exits, tps, vblk) * scale[:, :, None]
     average = jnp.sum(_gather_small(jnp.sum(student * halfgap, axis=2), "tensor", tensors), axis=0)
     grad_logits = (
         weights[:, None, None] * student * (halfgap - average[:, :, None])

time: 293 us -> 294 us (level)
    unnamed x13 -> x9, local copies, waits for them, and re-layouts: 9.25 us -> 9.24 us
  transfers between devices with their start and end apart: 5 -> 5, of which waited for: 5 -> 5; matrix products, arithmetic and copies ran while one was open for 8% -> 7% of each run, Pallas kernels for 0% -> 0%
where the time goes in v9:
time: 294 us
  waiting for transfers between devices  151 us (51%)
  blocking collectives  46.6 us (16%)
  matrix products  29.6 us (10%)
  starting transfers between devices  23.1 us (8%)
  local copies, waits for them, and re-layouts  17.8 us (6%)
  between operations  14.8 us (5%)
  other arithmetic  11 us (4%)
    reduce_scatter x1, waiting for transfers between devices, local(): own = lax.psum_scatter(part, 'section', scatter_dimension=0, tiled=True)  71.3 us
    all_gather x1, waiting for transfers between devices, local(): piece = lax.all_gather(grad_logits, 'section', axis=1, tiled=True)  49.9 us
    optimization_barrier x1, blocking collectives, local(): own, weights = lax.optimization_barrier((own, weights))  27.4 us
    all_to_all x1, blocking collectives, local(): cols = lax.all_to_all(x, 'section', 0, 0, tiled=True)  19.1 us
    all_to_all x2, waiting for transfers between devices, _gather_small(): return lax.all_to_all(sent, axis, 0, 0, tiled=True)  16.1 us
    all_to_all x1, waiting for transfers between devices, local(): lax.all_to_all(row_grad.astype(jnp.bfloat16), 'tensor', 0, 0, tiled=True)  13.5 us
    all_to_all x2, starting transfers between devices, _gather_small(): return lax.all_to_all(sent, axis, 0, 0, tiled=True)  13.3 us
    dot_general x1, matrix products, local(): part = jnp.dot(lhs, head, preferred_element_type=jnp.float32)  10.3 us
  transfers between devices with their start and end apart: 5, of which 5 were waited for; matrix products, arithmetic and copies ran while one was open for 7% of the time, Pallas kernels for 0%

profile of v9, /device:TPU:8, one launch (start us, length us, event | category | flops | bytes accessed | tf_op | source)
XLA Modules:
  0.0 293.7 jit_solution(5621923882347807073)
XLA Ops:
  7.2 0.0 reduce-scatter.2.cloned.1.call-start
  7.2 1.6 copy.46
  8.8 0.6 copy.31
  9.4 19.1 %all_to_all.20 = bf16[16,64,512]{2,1,0:T(8,128)(2,1)S(1)} all-to-all(bf16[16,64,512]{2,1,0:T(8,128)(2,1)S(1)} %copy.31), channel_id=1, replica_groups=mesh['section'=16,'tensor'=16] {'section'}, dimensions={0} | all-to-all | bytes 2097152 | tf_op jit(solution)/shard_map/all_to_all | solution.py:24
  28.5 0.3 reshape.82
  28.8 0.5 copy.60
  29.3 0.3 reshape.83
  29.6 10.3 %fusion.21 = f32[1024,4096]{1,0:T(8,128)} fusion(bf16[1024,512]{1,0:T(8,128)(2,1)S(1)} %reshape.83, bf16[512,4096]{1,0:T(8,128)(2,1)} %param.4), kind=kOutput, calls=%fused_computation.37 | convolution fusion | flops 4294967296 | bytes 22020096 | tf_op jit(solution)/shard_map/dot_general | solution.py:27
  39.8 0.0 reduce-scatter.2.cloned.1.call-update
  40.5 0.6 dynamic-slice
  41.1 0.8 dynamic-update-slice
  41.9 27.4 %all-reduce = f32[16]{0:T(128)S(1)} all-reduce(f32[16]{0:T(128)S(1)} %dynamic-update-slice), channel_id=1, replica_groups=mesh['section'=16,'tensor'=16] {'section'}, use_global_device_ids=true, to_apply=%add | all-reduce | flops 16 | bytes 128 | tf_op jit(solution)/shard_map/optimization_barrier | solution.py:31
  69.3 71.3 %reduce-scatter.2.cloned.1.call-done = f32[64,4096]{1,0:T(8,128)} async-done(((f32[1024,4096]{1,0:T(8,128)}), f32[64,4096]{1,0:T(8,128)}) %reduce-scatter.2.cloned.1.call-update) | async-done | bytes 1048592 | tf_op jit(solution)/shard_map/reduce_scatter | solution.py:30
  140.6 1.5 reduce_max.18
  142.1 0.1 slice_multiply_fusion.1
  142.1 1.5 fusion.19
  143.7 1.1 exponential_reduce_fusion
  144.8 0.1 maximum_bitcast_fusion
  144.9 0.6 broadcast_in_dim.6
  145.5 9.8 %all-to-all-start.1 = ((f32[16,2,68]{2,1,0:T(2,128)}), f32[16,2,68]{2,1,0:T(2,128)S(1)}, u32[]{:S(2)}, u32[]{:S(2)}) async-start(f32[16,2,68]{2,1,0:T(2,128)} %broadcast_in_dim.6), calls=%async_computation.2 | async-start | bytes 32768 | tf_op jit(solution)/shard_map/all_to_all | solution.py:11
  155.3 0.2 sub.98.clone
  155.5 1.3 sub.106
  156.9 8.4 %all-to-all-done.1 = f32[16,2,68]{2,1,0:T(2,128)S(1)} async-done(((f32[16,2,68]{2,1,0:T(2,128)}), f32[16,2,68]{2,1,0:T(2,128)S(1)}, u32[]{:S(2)}, u32[]{:S(2)}) %all-to-all-start.1) | async-done | bytes 8736 | tf_op jit(solution)/shard_map/all_to_all | solution.py:11
  165.4 0.1 subtract_exponential_fusion.1
  165.5 0.1 slice.34
  165.5 0.1 slice.36
  165.6 0.1 sub.108
  165.7 3.2 %fusion.14 = (f32[64]{0:T(128)S(1)}, f32[64,4096]{1,0:T(8,128)}) fusion(f32[64,4096]{1,0:T(8,128)} %sub.106, f32[64,4096]{1,0:T(8,128)S(1)} %copy-done, f32[64]{0:T(128)S(1)} %sub.108, f32[64]{0:T(128)S(1)} %bitcast.40, f32[64]{0:T(128)S(1)} %reduce_max.18), kind=kLoop, calls=%fused_computation.16 | loop fusion | flops 3669952 | bytes 3146752 | tf_op jit(solution)/shard_map/reduce_sum | solution.py:52
  169.0 0.1 broadcast_in_dim.7
  169.1 0.1 copy.39
  169.1 0.6 broadcast_in_dim.8
  169.8 3.5 %all-to-all-start.2 = ((f32[16,16,4]{1,2,0:T(4,128)}), f32[16,16,4]{1,2,0:T(4,128)S(1)}, u32[]{:S(2)}, u32[]{:S(2)}) async-start(f32[16,16,4]{1,2,0:T(4,128)} %broadcast_in_dim.8), calls=%async_computation.3 | async-start | bytes 65536 | tf_op jit(solution)/shard_map/all_to_all | solution.py:11
  173.3 0.2 all-gather.2.cloned.1.call-start
  173.5 0.3 reshape.85
  173.8 0.1 copy.37
  173.9 0.1 mul.46
  174.0 1.5 reshape.84
  175.5 0.1 copy.34
  175.6 7.6 %all-to-all-done.2 = f32[16,16,4]{1,2,0:T(4,128)S(1)} async-done(((f32[16,16,4]{1,2,0:T(4,128)}), f32[16,16,4]{1,2,0:T(4,128)S(1)}, u32[]{:S(2)}, u32[]{:S(2)}) %all-to-all-start.2) | async-done | bytes 4128 | tf_op jit(solution)/shard_map/all_to_all | solution.py:11
  183.3 2.5 fusion.10
  185.7 49.9 %all-gather.2.cloned.1.call-done = bf16[16,64,4096]{2,0,1:T(8,128)(2,1)} async-done(((bf16[16,4,4096]{2,0,1:T(8,128)(2,1)}), bf16[16,64,4096]{2,0,1:T(8,128)(2,1)}) %all-gather.2.cloned.1.call-update) | async-done | bytes 8388624 | tf_op jit(solution)/shard_map/all_gather | solution.py:56
  235.7 9.1 %fusion.3 = bf16[16,64,512]{2,0,1:T(8,128)(2,1)S(1)} fusion(bf16[16,64,4096]{2,0,1:T(8,128)(2,1)} %all-gather.2.cloned.1.call-done, bf16[512,4096]{1,0:T(8,128)(2,1)} %param.4), kind=kOutput, calls=%fused_computation.7 | convolution fusion | flops 4295491584 | bytes 13631488 | tf_op jit(solution)/shard_map/dot_general | solution.py:61
  244.8 1.6 copy.40
  246.4 9.5 %all-to-all-start.3 = ((bf16[16,64,512]{2,1,0:T(8,128)(2,1)}), bf16[16,64,512]{2,1,0:T(8,128)(2,1)S(1)}, u32[]{:S(2)}, u32[]{:S(2)}) async-start(bf16[16,64,512]{2,1,0:T(8,128)(2,1)} %copy.40), calls=%async_computation.4 | async-start | bytes 2097152 | tf_op jit(solution)/shard_map/all_to_all | solution.py:64
  255.9 10.2 %fusion = bf16[512,4096]{0,1:T(8,128)(2,1)} fusion(bf16[16,64,4096]{2,0,1:T(8,128)(2,1)} %all-gather.2.cloned.1.call-done, bf16[16,64,512]{2,1,0:T(8,128)(2,1)S(1)} %all_to_all.20), kind=kOutput, calls=%fused_computation.1 | convolution fusion | flops 4297064448 | bytes 13631488 | tf_op jit(solution)/shard_map/dot_general | solution.py:58
  266.2 6.3 %copy.42 = bf16[512,4096]{1,0:T(8,128)(2,1)} copy(bf16[512,4096]{0,1:T(8,128)(2,1)} %fusion) | data formatting | bytes 8388608
  272.5 13.5 %all-to-all-done.3 = bf16[16,64,512]{2,1,0:T(8,128)(2,1)S(1)} async-done(((bf16[16,64,512]{2,1,0:T(8,128)(2,1)}), bf16[16,64,512]{2,1,0:T(8,128)(2,1)S(1)}, u32[]{:S(2)}, u32[]{:S(2)}) %all-to-all-start.3) | async-done | bytes 1048608 | tf_op jit(solution)/shard_map/all_to_all | solution.py:64
  286.0 0.8 convert_reduce_fusion
  (12 shorter events, 0.1 us)
Async XLA Ops:
  7.2 133.4 %reduce-scatter.2.cloned.1.call-start = ((), (), s32[]{:S(2)}) async-start(), calls=%async_computation.5 | async-start | bytes 17825792 | tf_op jit(solution)/shard_map/reduce_scatter | solution.py:30
  39.8 0.7 copy-start.1
  140.6 25.1 %copy-start = (f32[64,4096]{1,0:T(8,128)S(1)}, f32[64,4096]{1,0:T(8,128)}, u32[]{:S(2)}) copy-start(f32[64,4096]{1,0:T(8,128)} %reduce-scatter.2.cloned.1.call-done) | copy-start | bytes 3145732
  145.5 19.8 %all-to-all-start.1 = ((f32[16,2,68]{2,1,0:T(2,128)}), f32[16,2,68]{2,1,0:T(2,128)S(1)}, u32[]{:S(2)}, u32[]{:S(2)}) async-start(f32[16,2,68]{2,1,0:T(2,128)} %broadcast_in_dim.6), calls=%async_computation.2 | async-start | bytes 32768 | tf_op jit(solution)/shard_map/all_to_all | solution.py:11
  169.8 13.4 %all-to-all-start.2 = ((f32[16,16,4]{1,2,0:T(4,128)}), f32[16,16,4]{1,2,0:T(4,128)S(1)}, u32[]{:S(2)}, u32[]{:S(2)}) async-start(f32[16,16,4]{1,2,0:T(4,128)} %broadcast_in_dim.8), calls=%async_computation.3 | async-start | bytes 65536 | tf_op jit(solution)/shard_map/all_to_all | solution.py:11
  173.3 62.4 %all-gather.2.cloned.1.call-start = ((), (), s32[]{:S(2)}) async-start(), calls=%async_computation.6 | async-start | bytes 8912896 | tf_op jit(solution)/shard_map/all_gather | solution.py:56
  246.4 39.6 %all-to-all-start.3 = ((bf16[16,64,512]{2,1,0:T(8,128)(2,1)}), bf16[16,64,512]{2,1,0:T(8,128)(2,1)S(1)}, u32[]{:S(2)}, u32[]{:S(2)}) async-start(bf16[16,64,512]{2,1,0:T(8,128)(2,1)} %copy.40), calls=%async_computation.4 | async-start | bytes 2097152 | tf_op jit(solution)/shard_map/all_to_all | solution.py:64
Sparse Core Ops, SparseCore 0:
  40.0 100.5 reduce-scatter.1
  185.9 49.7 all-gather.1

commit v10 on v8

--- a/solution.py
+++ b/solution.py
@@ -47,10 +47,12 @@
     halfgap = 0.5 * jnp.log(2.0) - 0.5 * jax.nn.softplus(gap - delta[:, :, None])
     scale = jnp.exp(top - norm)[: exits * tps].reshape(exits, tps)
     student = shifted[: exits * tps].reshape(exits, tps, vblk) * scale[:, :, None]
-    average = jnp.sum(_gather_small(jnp.sum(student * halfgap, axis=2), "tensor", tensors), axis=0)
-    grad_logits = (
-        weights[:, None, None] * student * (halfgap - average[:, :, None])
-    ).astype(jnp.bfloat16)
+    weighted = weights[:, None, None] * student
+    lead = weighted * halfgap
+    partial_average = jnp.sum(student * halfgap, axis=2)
+    lead, weighted, partial_average = lax.optimization_barrier((lead, weighted, partial_average))
+    average = jnp.sum(_gather_small(partial_average, "tensor", tensors), axis=0)
+    grad_logits = (lead - average[:, :, None] * weighted).astype(jnp.bfloat16)
     piece = lax.all_gather(grad_logits, "section", axis=1, tiled=True)
 
     head_grad = lax.dot_general(

time: 293 us -> 295 us (level)
  blocking collectives: 46.6 us -> 60.1 us
  waiting for transfers between devices: 150 us -> 141 us
  starting transfers between devices: 23.1 us -> 19.4 us
    all_to_all x0 -> x1, blocking collectives: none -> 13.6 us  [_gather_small(): return lax.all_to_all(sent, axis, 0, 0, tiled=True)]
    all_to_all x2 -> x1, waiting for transfers between devices: 14.8 us -> 5.87 us  [_gather_small(): return lax.all_to_all(sent, axis, 0, 0, tiled=True)]
    all_to_all x2 -> x1, starting transfers between devices: 13.3 us -> 9.8 us  [_gather_small(): return lax.all_to_all(sent, axis, 0, 0, tiled=True)]
  transfers between devices with their start and end apart: 5 -> 4, of which waited for: 5 -> 4; matrix products, arithmetic and copies ran while one was open for 8% -> 7% of each run, Pallas kernels for 0% -> 0%
where the time goes in v10:
time: 295 us
  waiting for transfers between devices  141 us (48%)
  blocking collectives  60.1 us (20%)
  matrix products  29.6 us (10%)
  starting transfers between devices  19.4 us (7%)
  local copies, waits for them, and re-layouts  19.4 us (7%)
  between operations  14.8 us (5%)
  other arithmetic  10.6 us (4%)
    reduce_scatter x1, waiting for transfers between devices, local(): own = lax.psum_scatter(part, 'section', scatter_dimension=0, tiled=True)  71.3 us
    all_gather x1, waiting for transfers between devices, local(): piece = lax.all_gather(grad_logits, 'section', axis=1, tiled=True)  49.9 us
    optimization_barrier x1, blocking collectives, local(): own, weights = lax.optimization_barrier((own, weights))  27.4 us
    all_to_all x1, blocking collectives, local(): cols = lax.all_to_all(x, 'section', 0, 0, tiled=True)  19.1 us
    all_to_all x1, blocking collectives, _gather_small(): return lax.all_to_all(sent, axis, 0, 0, tiled=True)  13.6 us
    all_to_all x1, waiting for transfers between devices, local(): lax.all_to_all(row_grad.astype(jnp.bfloat16), 'tensor', 0, 0, tiled=True)  13.5 us
    dot_general x1, matrix products, local(): part = jnp.dot(lhs, head, preferred_element_type=jnp.float32)  10.3 us
    dot_general x1, matrix products, local(): lax.dot_general(cols, piece, (((0, 1), (0, 1)), ((), ())), preferred_elem...  10.2 us
  transfers between devices with their start and end apart: 4, of which 4 were waited for; matrix products, arithmetic and copies ran while one was open for 7% of the time, Pallas kernels for 0%

profile of v10, /device:TPU:8, one launch (start us, length us, event | category | flops | bytes accessed | tf_op | source)
XLA Modules:
  0.0 294.6 jit_solution(7284280913948569196)
XLA Ops:
  7.2 0.0 reduce-scatter.2.cloned.1.call-start
  7.2 1.6 copy.46
  8.8 0.6 copy.31
  9.4 19.1 %all_to_all.20 = bf16[16,64,512]{2,1,0:T(8,128)(2,1)S(1)} all-to-all(bf16[16,64,512]{2,1,0:T(8,128)(2,1)S(1)} %copy.31), channel_id=1, replica_groups=mesh['section'=16,'tensor'=16] {'section'}, dimensions={0} | all-to-all | bytes 2097152 | tf_op jit(solution)/shard_map/all_to_all | solution.py:24
  28.5 0.3 reshape.80
  28.8 0.5 copy.59
  29.3 0.3 reshape.81
  29.6 10.3 %fusion.20 = f32[1024,4096]{1,0:T(8,128)} fusion(bf16[1024,512]{1,0:T(8,128)(2,1)S(1)} %reshape.81, bf16[512,4096]{1,0:T(8,128)(2,1)} %param.4), kind=kOutput, calls=%fused_computation.33 | convolution fusion | flops 4294967296 | bytes 22020096 | tf_op jit(solution)/shard_map/dot_general | solution.py:27
  39.8 0.0 copy-done.1
  39.8 0.0 reduce-scatter.2.cloned.1.call-update
  40.5 0.0 copy-done.3
  40.5 0.6 dynamic-slice
  41.1 0.8 dynamic-update-slice
  41.9 27.4 %all-reduce = f32[16]{0:T(128)S(1)} all-reduce(f32[16]{0:T(128)S(1)} %dynamic-update-slice), channel_id=1, replica_groups=mesh['section'=16,'tensor'=16] {'section'}, use_global_device_ids=true, to_apply=%add | all-reduce | flops 16 | bytes 128 | tf_op jit(solution)/shard_map/optimization_barrier | solution.py:31
  69.3 71.3 %reduce-scatter.2.cloned.1.call-done = f32[64,4096]{1,0:T(8,128)} async-done(((f32[1024,4096]{1,0:T(8,128)}), f32[64,4096]{1,0:T(8,128)}) %reduce-scatter.2.cloned.1.call-update) | async-done | bytes 1048592 | tf_op jit(solution)/shard_map/reduce_scatter | solution.py:30
  140.6 1.0 slice_multiply_fusion
  141.6 1.4 fusion.16
  143.0 1.6 fusion.18
  144.6 0.6 broadcast_in_dim.4
  145.2 9.8 %all-to-all-start.1 = ((f32[16,2,68]{2,1,0:T(2,128)}), f32[16,2,68]{2,1,0:T(2,128)S(1)}, u32[]{:S(2)}, u32[]{:S(2)}) async-start(f32[16,2,68]{2,1,0:T(2,128)} %broadcast_in_dim.4), calls=%async_computation.2 | async-start | bytes 32768 | tf_op jit(solution)/shard_map/all_to_all | solution.py:11
  155.0 0.0 all-gather.2.cloned.1.call-start
  155.0 0.0 copy-done
  155.0 1.3 reshape.83
  156.3 1.2 sub.83.clone
  157.5 1.6 sub.91
  159.1 5.9 %all-to-all-done.1 = f32[16,2,68]{2,1,0:T(2,128)S(1)} async-done(((f32[16,2,68]{2,1,0:T(2,128)}), f32[16,2,68]{2,1,0:T(2,128)S(1)}, u32[]{:S(2)}, u32[]{:S(2)}) %all-to-all-start.1) | async-done | bytes 8736 | tf_op jit(solution)/shard_map/all_to_all | solution.py:11
  165.1 0.1 slice.34
  165.1 0.1 slice.36
  165.2 0.1 sub.93
  165.3 0.1 copy.37
  165.4 0.1 mul.54
  165.5 1.9 fusion.12
  167.4 1.5 reshape.82
  168.9 0.1 copy.34
  169.0 0.1 reduce_sum.50
  169.1 2.9 fusion.8
  172.0 0.1 copy.39
  172.1 13.6 %all_to_all.21 = f32[16,16,4]{1,2,0:T(4,128)S(1)} all-to-all(f32[16,16,4]{1,2,0:T(4,128)S(1)} %broadcast_in_dim.5), channel_id=1, replica_groups=mesh['section'=16,'tensor'=16] {'tensor'}, dimensions={0} | all-to-all | bytes 8192 | tf_op jit(solution)/shard_map/all_to_all | solution.py:11
  185.6 1.0 subtract_convert_fusion
  186.6 0.0 all-gather.2.cloned.1.call-update
  186.6 49.9 %all-gather.2.cloned.1.call-done = bf16[16,64,4096]{2,0,1:T(8,128)(2,1)} async-done(((bf16[16,4,4096]{2,0,1:T(8,128)(2,1)}), bf16[16,64,4096]{2,0,1:T(8,128)(2,1)}) %all-gather.2.cloned.1.call-update) | async-done | bytes 8388624 | tf_op jit(solution)/shard_map/all_gather | solution.py:56
  236.5 9.1 %fusion.3 = bf16[16,64,512]{2,0,1:T(8,128)(2,1)S(1)} fusion(bf16[16,64,4096]{2,0,1:T(8,128)(2,1)} %all-gather.2.cloned.1.call-done, bf16[512,4096]{1,0:T(8,128)(2,1)} %param.4), kind=kOutput, calls=%fused_computation.7 | convolution fusion | flops 4295491584 | bytes 13631488 | tf_op jit(solution)/shard_map/dot_general | solution.py:61
  245.6 1.6 copy.40
  247.3 9.5 %all-to-all-start.3 = ((bf16[16,64,512]{2,1,0:T(8,128)(2,1)}), bf16[16,64,512]{2,1,0:T(8,128)(2,1)S(1)}, u32[]{:S(2)}, u32[]{:S(2)}) async-start(bf16[16,64,512]{2,1,0:T(8,128)(2,1)} %copy.40), calls=%async_computation.4 | async-start | bytes 2097152 | tf_op jit(solution)/shard_map/all_to_all | solution.py:64
  256.8 10.2 %fusion = bf16[512,4096]{0,1:T(8,128)(2,1)} fusion(bf16[16,64,4096]{2,0,1:T(8,128)(2,1)} %all-gather.2.cloned.1.call-done, bf16[16,64,512]{2,1,0:T(8,128)(2,1)S(1)} %copy-done.2), kind=kOutput, calls=%fused_computation.1 | convolution fusion | flops 4297064448 | bytes 13631488 | tf_op jit(solution)/shard_map/dot_general | solution.py:58
  267.1 6.3 %copy.42 = bf16[512,4096]{1,0:T(8,128)(2,1)} copy(bf16[512,4096]{0,1:T(8,128)(2,1)} %fusion) | data formatting | bytes 8388608
  273.4 13.5 %all-to-all-done.3 = bf16[16,64,512]{2,1,0:T(8,128)(2,1)S(1)} async-done(((bf16[16,64,512]{2,1,0:T(8,128)(2,1)}), bf16[16,64,512]{2,1,0:T(8,128)(2,1)S(1)}, u32[]{:S(2)}, u32[]{:S(2)}) %all-to-all-start.3) | async-done | bytes 1048608 | tf_op jit(solution)/shard_map/all_to_all | solution.py:64
  286.9 0.8 convert_reduce_fusion
  (14 shorter events, 0.1 us)
Async XLA Ops:
  7.2 133.4 %reduce-scatter.2.cloned.1.call-start = ((), (), s32[]{:S(2)}) async-start(), calls=%async_computation.5 | async-start | bytes 17825792 | tf_op jit(solution)/shard_map/reduce_scatter | solution.py:30
  28.5 11.3 %copy-start.1 = (bf16[16,64,512]{2,1,0:T(8,128)(2,1)}, bf16[16,64,512]{2,1,0:T(8,128)(2,1)S(1)}, u32[]{:S(2)}) copy-start(bf16[16,64,512]{2,1,0:T(8,128)(2,1)S(1)} %all_to_all.20) | copy-start | bytes 3145732
  39.8 0.7 copy-start.3
  140.6 14.5 %copy-start = (f32[64,4096]{1,0:T(8,128)S(1)}, f32[64,4096]{1,0:T(8,128)}, u32[]{:S(2)}) copy-start(f32[64,4096]{1,0:T(8,128)} %reduce-scatter.2.cloned.1.call-done) | copy-start | bytes 3145732
  145.2 19.8 %all-to-all-start.1 = ((f32[16,2,68]{2,1,0:T(2,128)}), f32[16,2,68]{2,1,0:T(2,128)S(1)}, u32[]{:S(2)}, u32[]{:S(2)}) async-start(f32[16,2,68]{2,1,0:T(2,128)} %broadcast_in_dim.4), calls=%async_computation.2 | async-start | bytes 32768 | tf_op jit(solution)/shard_map/all_to_all | solution.py:11
  155.0 81.5 %all-gather.2.cloned.1.call-start = ((), (), s32[]{:S(2)}) async-start(), calls=%async_computation.6 | async-start | bytes 8912896 | tf_op jit(solution)/shard_map/all_gather | solution.py:56
  245.6 11.2 %copy-start.2 = (bf16[16,64,512]{2,1,0:T(8,128)(2,1)S(1)}, bf16[16,64,512]{2,1,0:T(8,128)(2,1)}, u32[]{:S(2)}) copy-start(bf16[16,64,512]{2,1,0:T(8,128)(2,1)} %copy-done.1) | copy-start | bytes 3145732
  247.3 39.6 %all-to-all-start.3 = ((bf16[16,64,512]{2,1,0:T(8,128)(2,1)}), bf16[16,64,512]{2,1,0:T(8,128)(2,1)S(1)}, u32[]{:S(2)}, u32[]{:S(2)}) async-start(bf16[16,64,512]{2,1,0:T(8,128)(2,1)} %copy.40), calls=%async_computation.4 | async-start | bytes 2097152 | tf_op jit(solution)/shard_map/all_to_all | solution.py:64
Sparse Core Ops, SparseCore 0:
  40.0 100.5 reduce-scatter.1
  186.8 49.7 all-gather.1
